TPU v7x, 128 devices: a whole 4x4x4 slice. The times are simulated.
128 devices in a mesh: grp: 8 (over z_lo, x), blk: 16 (over z_hi, y, core).
Axes of the slice: x: 4, y: 4, z: 4 (z_hi: 2, z_lo: 2; z = z_hi * 2 + z_lo), core: 2. Of those that a mesh axis runs over, the one named last changes fastest.
Arguments:
- matrix: bfloat16 [16384, 16384], P('blk', 'grp')
- panels: bfloat16 [16384, 4096], P('grp', 'blk')
- pattern: int32 [128, 128], replicated, may hold values from 0 to 1, as said below
- pruned: int32 [128, 32], replicated, may hold values from 0 to 1, as said below
- owners: int32 [32], replicated, may hold values from 0 to 31, each once
Outputs:
- owned: float32 [16, 8, 128, 4096], P(None, 'grp', None, 'blk')
Inputs may be any that keep to these rules, and one draw needn't show every extreme that they name: `pattern`: 0 or 1; every diagonal block is 1. `pruned`: 0 or 1; block (c, c) is 1 for every window column block c; every block row holds exactly 16 ones. `owners`: each slot once.
All inputs are finite; a program needn't handle non-finite values.
Results may differ from a plain program's by a relative error of at most 0.0003.
Values may be sent and summed in bfloat16 or wider, within the bound.
No kernel may reach another device: no remote copies, remote signals or barrier semaphores. Data moves between devices by JAX's collectives and lax.ppermute only.
A program may use at most 128 MiB of HBM per device.

v0:
```python
import jax
import jax.numpy as jnp
from jax import lax
from jax.sharding import Mesh
from jax.sharding import PartitionSpec as P

BS = 128
BLK = ("blk_0", "blk_1", "blk_2")
GRP = ("grp_0", "grp_1")
GRP_BLK = ("grp_0", "grp_1", "blk_0", "blk_1", "blk_2")


def by_axis(x, axes):
    for axis in axes:
        x = lax.psum(x, axis)
    return x


def shards(matrix, panels, pattern, pruned, owners):
    blk_count = lax.axis_size(BLK)
    blk_id = lax.axis_index(BLK)
    grp_id = lax.axis_index(GRP)
    row_count, inner = matrix.shape
    panel_width = panels.shape[1]
    row_blocks = row_count // BS
    inner_blocks = inner // BS
    panel_blocks = panel_width // BS
    width_total = panel_width * blk_count
    window_blocks = width_total // BS
    half_blocks = window_blocks // 2
    tile_left = lax.dynamic_slice(
        pattern, (blk_id * row_blocks, grp_id * inner_blocks), (row_blocks, inner_blocks)
    ).astype(jnp.bfloat16)
    left = (matrix.reshape(row_blocks, BS, inner_blocks, BS) * tile_left[:, None, :, None]).reshape(
        row_count, inner
    )
    tile_right = lax.dynamic_slice(
        pattern, (grp_id * inner_blocks, blk_id * panel_blocks), (inner_blocks, panel_blocks)
    ).astype(jnp.bfloat16)
    right = (
        panels.reshape(inner_blocks, BS, panel_blocks, BS) * tile_right[:, None, :, None]
    ).reshape(inner, panel_width)
    partial_value = jnp.dot(
        left, lax.all_gather(right, BLK, axis=1, tiled=True), preferred_element_type=jnp.float32
    )
    piece_rows = row_count // lax.axis_size(GRP)
    first_row = blk_id * row_count + grp_id * piece_rows
    row_block = (first_row + jnp.arange(piece_rows, dtype=jnp.int32)) // BS
    select = (row_block[:, None] == jnp.arange(pattern.shape[0], dtype=jnp.int32)[None, :]).astype(
        jnp.float32
    )
    keep_mask = jnp.dot(select, pruned.astype(jnp.float32), precision=lax.Precision.HIGHEST)
    local_pruned = lax.dynamic_slice_in_dim(pruned, blk_id * row_blocks, row_blocks, 0)
    column_ids = jnp.arange(window_blocks, dtype=jnp.int32)
    listing = jnp.argsort((1 - local_pruned) * window_blocks + column_ids[None, :], axis=1)[
        :, :half_blocks
    ]
    blocked = partial_value.reshape(row_blocks, BS, window_blocks, BS)
    packed = jnp.take_along_axis(blocked, listing[:, None, :, None], axis=2).reshape(
        row_count, half_blocks * BS
    )
    summed_packed = lax.psum_scatter(packed, GRP, scatter_dimension=0, tiled=True)
    slot_of = jnp.clip(jnp.cumsum(pruned, axis=1) - 1, 0, half_blocks - 1)
    row_slots = jnp.dot(
        select, slot_of.astype(jnp.float32), precision=lax.Precision.HIGHEST
    ).astype(jnp.int32)
    summed = jnp.take_along_axis(
        summed_packed.reshape(piece_rows, half_blocks, BS), row_slots[:, :, None], axis=1
    )
    inflated = summed * summed
    kept = (inflated * keep_mask[:, :, None]).reshape(piece_rows, width_total)
    totals = by_axis(jnp.sum(kept, axis=0), GRP_BLK)
    normalized = row_count * blk_count * kept / totals
    inverse = (
        jnp.zeros((window_blocks,), jnp.int32)
        .at[owners]
        .set(jnp.arange(window_blocks, dtype=jnp.int32))
    )
    arranged = normalized.reshape(piece_rows, window_blocks, BS)[:, inverse, :].reshape(
        1, piece_rows, width_total
    )
    moved = lax.all_to_all(arranged, BLK, split_axis=2, concat_axis=0, tiled=True)
    return moved[:, None, :, :]


def solution(mesh):
    split = Mesh(mesh.devices.reshape(2, 4, 2, 4, 2), ("grp_0", "grp_1", "blk_0", "blk_1", "blk_2"))
    placed = (P(BLK, GRP), P(GRP, BLK), P(), P(), P())
    return jax.shard_map(
        shards, mesh=split, in_specs=placed, out_specs=P(None, GRP, None, BLK), check_vma=False
    )
```

profile of v0, /device:TPU:2, one launch (start us, length us, event | category | flops | bytes accessed | tf_op | source)
XLA Modules:
  0.0 429.4 jit_solution(4213240560578115987)
XLA Ops:
  7.9 2.4 bitcast_multiply_fusion.1
  10.5 0.8 sort.17
  12.9 1.6 copy-done
  14.5 3.0 bitcast_multiply_fusion
  17.5 117.7 %all-gather.2.cloned.1.call-done = bf16[2048,4096]{1,0:T(8,128)(2,1)} async-done(((bf16[2048,256]{1,0:T(8,128)(2,1)}), bf16[2048,4096]{1,0:T(8,128)(2,1)}) %all-gather.2.cloned.1.call-update) | async-done | bytes 16777232 | tf_op jit(solution)/shard_map/all_gather | solution.py:44
  135.2 22.6 %copy.25 = bf16[4096,2048]{1,0:T(8,128)(2,1)} copy(bf16[4096,2048]{0,1:T(8,128)(2,1)} %bitcast.53) | data formatting | bytes 33554432 | tf_op jit(solution)/shard_map/dot_general | solution.py:43
  157.7 23.6 %fusion.18 = f32[8,128,32,128]{3,1,2,0:T(8,128)} fusion(bf16[8,128,2048,1]{2,1,3,0:T(8,128)(2,1)} %bitcast.58, bf16[32,128,2048,1]{2,1,0,3:T(8,128)(2,1)} %bitcast.54), kind=kOutput, calls=%fused_computation.47 | convolution fusion | flops 17179869184 | bytes 37748736 | tf_op jit(solution)/shard_map/dot_general | solution.py:43
  181.3 10.1 %gather_fusion.1 = f32[128,128,128]{2,1,0:T(8,128)} fusion(f32[8,128,32,128]{3,1,2,0:T(8,128)} %fusion.18, s32[128]{0:T(128)S(1)} %reshape.94), kind=kCustom, calls=%fused_computation.1 | custom fusion | bytes 16778240 | tf_op jit(solution)/shard_map/jit(take_along_axis)/gather | solution.py:59
  191.4 9.1 %copy_select_fusion = f32[8,16,128,128]{3,1,2,0:T(8,128)S(1)} fusion(f32[8,16,128,128]{3,2,1,0:T(8,128)} %bitcast.48, pred[8,16]{1,0:T(8,128)(4,1)S(1)} %copy.24), kind=kLoop, calls=%fused_computation.5 | loop fusion | flops 2097152 | bytes 16777344 | tf_op jit(solution)/shard_map/jit(take_along_axis)/select_n | solution.py:59
  200.5 7.3 %copy.51 = f32[128,8,16,128]{3,1,2,0:T(8,128)} copy(f32[128,8,16,128]{3,2,1,0:T(8,128)S(1)} %bitcast.49) | data formatting | bytes 16777216
  209.4 87.0 %reduce-scatter.2.cloned.1.call-done = f32[128,2048]{1,0:T(8,128)} async-done(((f32[1024,2048]{1,0:T(8,128)}), f32[128,2048]{1,0:T(8,128)}) %reduce-scatter.2.cloned.1.call-update) | async-done | bytes 1048592 | tf_op jit(solution)/shard_map/reduce_scatter | solution.py:62
  296.4 1.4 copy.37
  297.8 25.8 %gather_fusion.2 = f32[4096,128]{1,0:T(8,128)S(1)} fusion(f32[128,16,128]{2,1,0:T(8,128)S(1)} %bitcast.46, s32[4096]{0:T(1024)S(1)} %reshape.100), kind=kCustom, calls=%fused_computation.2 | custom fusion | bytes 4227072 | tf_op jit(solution)/shard_map/jit(take_along_axis)/gather | solution.py:67
  323.6 2.4 fusion.2
  326.0 8.3 %psum.35 = f32[4096]{0:T(1024)S(1)} all-reduce(f32[4096]{0:T(1024)S(1)} %bitcast.61), channel_id=1, replica_groups=mesh['grp_0'=2,'grp_1'=4,'blk_0'=2,'blk_1'=4,'blk_2'=2] {'grp_0'}, use_global_device_ids=true, to_apply=%region_4.5 | all-reduce | flops 4096 | bytes 32768 | tf_op jit(solution)/shard_map/psum | solution.py:15
  334.3 14.5 %psum.36 = f32[4096]{0:T(1024)S(1)} all-reduce(f32[4096]{0:T(1024)S(1)} %psum.35), channel_id=1, replica_groups=mesh['grp_0'=2,'grp_1'=4,'blk_0'=2,'blk_1'=4,'blk_2'=2] {'grp_1'}, use_global_device_ids=true, to_apply=%region_5.6 | all-reduce | flops 4096 | bytes 32768 | tf_op jit(solution)/shard_map/psum | solution.py:15
  348.9 11.3 %psum.37 = f32[4096]{0:T(1024)S(1)} all-reduce(f32[4096]{0:T(1024)S(1)} %psum.36), channel_id=1, replica_groups=mesh['grp_0'=2,'grp_1'=4,'blk_0'=2,'blk_1'=4,'blk_2'=2] {'blk_0'}, use_global_device_ids=true, to_apply=%region_6.7 | all-reduce | flops 4096 | bytes 32768 | tf_op jit(solution)/shard_map/psum | solution.py:15
  360.2 16.9 %psum.38 = f32[4096]{0:T(1024)S(1)} all-reduce(f32[4096]{0:T(1024)S(1)} %psum.37), channel_id=1, replica_groups=mesh['grp_0'=2,'grp_1'=4,'blk_0'=2,'blk_1'=4,'blk_2'=2] {'blk_1'}, use_global_device_ids=true, to_apply=%region_7.8 | all-reduce | flops 4096 | bytes 32768 | tf_op jit(solution)/shard_map/psum | solution.py:15
  377.0 3.3 psum.39
  380.4 3.5 multiply_divide_fusion
  383.8 2.3 gather_fusion
  386.1 1.8 copy.30
  387.9 32.9 %all_to_all.15 = f32[1,128,4096]{1,0,2:T(1,128)S(1)} all-to-all(f32[1,128,4096]{1,0,2:T(1,128)} %bitcast.56), channel_id=1, replica_groups=mesh['grp_0'=2,'grp_1'=4,'blk_0'=2,'blk_1'=4,'blk_2'=2] {'blk_0','blk_1'..., dimensions={2} | all-to-all | bytes 4194304 | tf_op jit(solution)/shard_map/all_to_all | solution.py:82
  420.8 1.8 copy.32
  (33 shorter events, 4.7 us)
Async XLA Ops:
  6.5 128.6 %all-gather.2.cloned.1.call-start = ((), (), s32[]{:S(2)}) async-start(), calls=%async_computation.2 | async-start | bytes 17825792 | tf_op jit(solution)/shard_map/all_gather | solution.py:44
  7.9 2.5 copy-start.1
  10.3 286.1 %reduce-scatter.2.cloned.1.call-start = ((), (), s32[]{:S(2)}) async-start(), calls=%async_computation.3 | async-start | bytes 9437184 | tf_op jit(solution)/shard_map/reduce_scatter | solution.py:62
  12.3 2.2 copy-start
  207.8 0.7 copy-start.2
Sparse Core Ops, SparseCore 0:
  10.5 124.6 all-gather.1
  208.0 88.3 reduce-scatter.1
where the time goes:
time: 432 us; the launch traced here: 429 us
  waiting for transfers between devices  205 us (47%)
  blocking collectives  87.2 us (20%)
  local copies, waits for them, and re-layouts  77.1 us (18%)
  matrix products  24 us (6%)
  other arithmetic  22.9 us (5%)
  between operations  13.5 us (3%)
    all_gather x1, waiting for transfers between devices, shards(): lax.all_gather(right, BLK, axis=1, tiled=True)  118 us
    reduce_scatter x1, waiting for transfers between devices, shards(): lax.psum_scatter(packed, GRP, scatter_dimension=0, tiled=True)  87 us
    psum x5, blocking collectives, by_axis(): x = lax.psum(x, axis)  54.3 us
    all_to_all x1, blocking collectives, shards(): lax.all_to_all(arranged, BLK, split_axis=2, concat_axis=0, tiled=True)  32.9 us
    gather x3, local copies, waits for them, and re-layouts, shards(): jnp.take_along_axis(summed_packed.reshape(piece_rows, half_blocks, BS), r...  26 us
    dot_general x1, matrix products, shards(): jnp.dot(left, lax.all_gather(right, BLK, axis=1, tiled=True), preferred_e...  23.6 us
    dot_general x1, local copies, waits for them, and re-layouts, shards(): jnp.dot(left, lax.all_gather(right, BLK, axis=1, tiled=True), preferred_e...  22.6 us
    unnamed x8, local copies, waits for them, and re-layouts  10.4 us
  transfers between devices with their start and end apart: 2, of which 2 were waited for; matrix products, arithmetic and copies ran while one was open for 2% of the time, Pallas kernels for 0%

commit v1 on v0

v1 whole, which is shorter than its diff:
```python
import jax
import jax.numpy as jnp
from jax import lax
from jax.sharding import Mesh
from jax.sharding import PartitionSpec as P

BS = 128
BLK = ("blk_0", "blk_1", "blk_2")
GRP = ("grp_0", "grp_1")
GRP_BLK = ("grp_0", "grp_1", "blk_0", "blk_1", "blk_2")
REMOTE = ("blk_0", "blk_1")
CORE = "blk_2"


def shards(matrix, panels, pattern, pruned, owners):
    blk_count = lax.axis_size(BLK)
    blk_id = lax.axis_index(BLK)
    grp_id = lax.axis_index(GRP)
    core_count = lax.axis_size(CORE)
    remote_count = lax.axis_size(REMOTE)
    row_count, inner = matrix.shape
    panel_width = panels.shape[1]
    row_blocks = row_count // BS
    inner_blocks = inner // BS
    panel_blocks = panel_width // BS
    width_total = panel_width * blk_count
    window_blocks = width_total // BS
    half_blocks = window_blocks // 2
    tile_left = lax.dynamic_slice(
        pattern, (blk_id * row_blocks, grp_id * inner_blocks), (row_blocks, inner_blocks)
    ).astype(jnp.bfloat16)
    left = (matrix.reshape(row_blocks, BS, inner_blocks, BS) * tile_left[:, None, :, None]).reshape(
        row_count, inner
    )
    tile_right = lax.dynamic_slice(
        pattern, (grp_id * inner_blocks, blk_id * panel_blocks), (inner_blocks, panel_blocks)
    ).astype(jnp.bfloat16)
    right = (
        panels.reshape(inner_blocks, BS, panel_blocks, BS) * tile_right[:, None, :, None]
    ).reshape(inner, panel_width)
    gathered = lax.all_gather(right, REMOTE, axis=1, tiled=True)
    gathered = lax.all_gather(gathered, CORE, axis=1, tiled=True)
    column_ids = jnp.arange(window_blocks, dtype=jnp.int32)
    src_blk = column_ids // panel_blocks
    position = (
        (src_blk % core_count) * remote_count + src_blk // core_count
    ) * panel_blocks + column_ids % panel_blocks
    partial_value = jnp.dot(left, gathered, preferred_element_type=jnp.float32)
    local_pruned = lax.dynamic_slice_in_dim(pruned, blk_id * row_blocks, row_blocks, 0)
    listing = jnp.argsort((1 - local_pruned) * window_blocks + column_ids[None, :], axis=1)[
        :, :half_blocks
    ]
    blocked = partial_value.reshape(row_blocks, BS, window_blocks, BS)
    packed = jnp.take_along_axis(blocked, position[listing][:, None, :, None], axis=2).reshape(
        row_count, half_blocks * BS
    )
    summed_packed = lax.psum_scatter(packed, GRP, scatter_dimension=0, tiled=True)
    piece_rows = row_count // lax.axis_size(GRP)
    row_block = (blk_id * row_count + grp_id * piece_rows) // BS
    row_pruned = lax.dynamic_index_in_dim(pruned, row_block, 0, keepdims=False)
    slot_of = jnp.clip(jnp.cumsum(row_pruned) - 1, 0, half_blocks - 1)
    squared = summed_packed.reshape(piece_rows, half_blocks, BS)
    squared = squared * squared
    local_totals = jnp.sum(squared, axis=0)[slot_of] * row_pruned.astype(jnp.float32)[:, None]
    totals = lax.psum(local_totals, GRP_BLK)
    inverse = (
        jnp.zeros((window_blocks,), jnp.int32)
        .at[owners]
        .set(jnp.arange(window_blocks, dtype=jnp.int32))
    )
    picked = jnp.take(squared, slot_of[inverse], axis=1)
    kept = picked * row_pruned[inverse].astype(jnp.float32)[None, :, None]
    normalized = (row_count * blk_count) * kept / totals[inverse][None, :, :]
    arranged = normalized.reshape(1, piece_rows, width_total)
    moved = lax.all_to_all(arranged, BLK, split_axis=2, concat_axis=0, tiled=True)
    return moved[:, None, :, :]


def solution(mesh):
    split = Mesh(mesh.devices.reshape(2, 4, 2, 4, 2), ("grp_0", "grp_1", "blk_0", "blk_1", "blk_2"))
    placed = (P(BLK, GRP), P(GRP, BLK), P(), P(), P())
    return jax.shard_map(
        shards, mesh=split, in_specs=placed, out_specs=P(None, GRP, None, BLK), check_vma=False
    )
```

time: 432 us -> 449 us (1.039)
  waiting for transfers between devices: 205 us -> 235 us
  local copies, waits for them, and re-layouts: 77.1 us -> 54.5 us
  blocking collectives: 87.2 us -> 99.7 us
    all_gather x1 -> x2, waiting for transfers between devices: 118 us -> 147 us  [the longest x1 122 us: shards(): gathered = lax.all_gather(right, REMOTE, axis=1, tiled=True)]
    gather x8 -> x13, local copies, waits for them, and re-layouts: 40.3 us -> 18.2 us  [the longest x2 10.2 us: shards(): jnp.take_along_axis(blocked, position[listing][:, None, :, None], axis=2)]
    psum x5 -> x1, blocking collectives: 54.3 us -> 66.2 us  [shards(): totals = lax.psum(local_totals, GRP_BLK)]
    unnamed x8 -> x7, local copies, waits for them, and re-layouts: 10.4 us -> 8.65 us
    dot_general x3 -> x1, matrix products: 24 us -> 23.6 us  [shards(): partial_value = jnp.dot(left, gathered, preferred_element_type=jnp.float32)]
    select_n x3 -> x5, other arithmetic: 9.12 us -> 9.35 us  [the longest x1 9.11 us: shards(): jnp.take_along_axis(blocked, position[listing][:, None, :, None], axis=2)]
  transfers between devices with their start and end apart: 2 -> 3, of which waited for: 2 -> 3; matrix products, arithmetic and copies ran while one was open for 2% -> 2% of each run, Pallas kernels for 0% -> 0%
where the time goes in v1:
time: 449 us; the launch traced here: 448 us
  waiting for transfers between devices  235 us (52%)
  blocking collectives  99.7 us (22%)
  local copies, waits for them, and re-layouts  54.5 us (12%)
  matrix products  23.6 us (5%)
  other arithmetic  20.9 us (5%)
  between operations  13.3 us (3%)
    all_gather x1, waiting for transfers between devices, shards(): gathered = lax.all_gather(right, REMOTE, axis=1, tiled=True)  122 us
    reduce_scatter x1, waiting for transfers between devices, shards(): lax.psum_scatter(packed, GRP, scatter_dimension=0, tiled=True)  88.8 us
    psum x1, blocking collectives, shards(): totals = lax.psum(local_totals, GRP_BLK)  66.2 us
    all_to_all x1, blocking collectives, shards(): lax.all_to_all(arranged, BLK, split_axis=2, concat_axis=0, tiled=True)  33.5 us
    all_gather x1, waiting for transfers between devices, shards(): gathered = lax.all_gather(gathered, CORE, axis=1, tiled=True)  24.5 us
    dot_general x1, matrix products, shards(): partial_value = jnp.dot(left, gathered, preferred_element_type=jnp.float32)  23.6 us
    dot_general x1, local copies, waits for them, and re-layouts, shards(): partial_value = jnp.dot(left, gathered, preferred_element_type=jnp.float32)  22.6 us
    gather x2, local copies, waits for them, and re-layouts, shards(): jnp.take_along_axis(blocked, position[listing][:, None, :, None], axis=2)  10.2 us
  transfers between devices with their start and end apart: 3, of which 3 were waited for; matrix products, arithmetic and copies ran while one was open for 2% of the time, Pallas kernels for 0%

profile of v1, /device:TPU:2, one launch (start us, length us, event | category | flops | bytes accessed | tf_op | source)
XLA Modules:
  0.0 447.6 jit_solution(1881725267968182274)
XLA Ops:
  6.5 0.8 dynamic-slice_convert_fusion
  7.9 2.4 bitcast_multiply_fusion.1
  10.4 122.1 %all-gather.3.cloned.1.call-done = bf16[2048,2048]{1,0:T(8,128)(2,1)} async-done(((bf16[2048,256]{1,0:T(8,128)(2,1)}), bf16[2048,2048]{1,0:T(8,128)(2,1)}) %all-gather.3.cloned.1.call-update) | async-done | bytes 8388624 | tf_op jit(solution)/shard_map/all_gather | solution.py:41
  133.3 0.8 sort.17
  134.3 1.2 gather_fusion.1
  135.9 0.9 dynamic-slice_convert_fusion.1
  138.1 3.0 bitcast_multiply_fusion
  141.1 24.5 %all-gather.5.cloned.1.call-done = bf16[2048,4096]{1,0:T(8,128)(2,1)} async-done(((bf16[2048,2048]{1,0:T(8,128)(2,1)}), bf16[2048,4096]{1,0:T(8,128)(2,1)}) %all-gather.5.cloned.1.call-update) | async-done | bytes 16777232 | tf_op jit(solution)/shard_map/all_gather | solution.py:42
  165.6 22.6 %copy.44 = bf16[4096,2048]{1,0:T(8,128)(2,1)} copy(bf16[4096,2048]{0,1:T(8,128)(2,1)} %bitcast.55) | data formatting | bytes 33554432 | tf_op jit(solution)/shard_map/dot_general | solution.py:48
  188.2 23.6 %fusion.14 = f32[8,128,32,128]{3,1,2,0:T(8,128)} fusion(bf16[8,128,2048,1]{2,1,3,0:T(8,128)(2,1)} %bitcast.60, bf16[32,128,2048,1]{2,1,0,3:T(8,128)(2,1)} %bitcast.56), kind=kOutput, calls=%fused_computation.61 | convolution fusion | flops 17179869184 | bytes 37748736 | tf_op jit(solution)/shard_map/dot_general | solution.py:48
  211.7 10.1 %gather_fusion.6 = f32[128,128,128]{2,1,0:T(8,128)} fusion(f32[8,128,32,128]{3,1,2,0:T(8,128)} %fusion.14, s32[128]{0:T(128)S(1)} %reshape.228), kind=kCustom, calls=%fused_computation.6 | custom fusion | bytes 16778240 | tf_op jit(solution)/shard_map/jit(take_along_axis)/gather | solution.py:54
  221.8 9.1 %copy_select_fusion = f32[8,16,128,128]{3,1,2,0:T(8,128)S(1)} fusion(f32[8,16,128,128]{3,2,1,0:T(8,128)} %bitcast.52, pred[8,16]{1,0:T(8,128)(4,1)S(1)} %copy.43), kind=kLoop, calls=%fused_computation.9 | loop fusion | flops 2097152 | bytes 16777344 | tf_op jit(solution)/shard_map/jit(take_along_axis)/select_n | solution.py:54
  230.9 7.3 %copy.62 = f32[128,8,16,128]{3,1,2,0:T(8,128)} copy(f32[128,8,16,128]{3,2,1,0:T(8,128)S(1)} %bitcast.53) | data formatting | bytes 16777216
  238.6 0.9 scatter_custom_fusion
  239.5 0.7 gather_fusion.3
  240.3 0.7 gather_fusion
  241.4 88.8 %reduce-scatter.2.cloned.1.call-done = f32[128,2048]{1,0:T(8,128)} async-done(((f32[1024,2048]{1,0:T(8,128)}), f32[128,2048]{1,0:T(8,128)}) %reduce-scatter.2.cloned.1.call-update) | async-done | bytes 1048592 | tf_op jit(solution)/shard_map/reduce_scatter | solution.py:57
  330.2 1.4 multiply_reduce_fusion
  332.3 2.0 gather_fusion.2
  334.3 1.9 copy.51
  336.8 66.2 %psum.7 = f32[32,128]{1,0:T(8,128)S(1)} all-reduce(f32[32,128]{1,0:T(8,128)S(1)} %broadcast_multiply_fusion), channel_id=1, replica_groups=mesh['grp_0'=2,'grp_1'=4,'blk_0'=2,'blk_1'=4,'blk_2'=2] {'grp_0','grp_1'..., use_global_device_ids=true, to_apply=%region_5.6 | all-reduce | flops 4096 | bytes 32768 | tf_op jit(solution)/shard_map/psum | solution.py:65
  403.6 2.1 fusion.2
  405.7 33.5 %all_to_all.15 = f32[1,128,4096]{1,0,2:T(1,128)S(1)} all-to-all(f32[1,128,4096]{1,0,2:T(1,128)S(1)} %bitcast.57), channel_id=1, replica_groups=mesh['grp_0'=2,'grp_1'=4,'blk_0'=2,'blk_1'=4,'blk_2'=2] {'blk_0','blk_1'..., dimensions={2} | all-to-all | bytes 4194304 | tf_op jit(solution)/shard_map/all_to_all | solution.py:75
  439.3 1.8 copy.53
  (48 shorter events, 6.0 us)
Async XLA Ops:
  6.5 125.9 %all-gather.3.cloned.1.call-start = ((), (), s32[]{:S(2)}) async-start(), calls=%async_computation.2 | async-start | bytes 9437184 | tf_op jit(solution)/shard_map/all_gather | solution.py:41
  10.3 155.3 %all-gather.5.cloned.1.call-start = ((), (), s32[]{:S(2)}) async-start(), calls=%async_computation.3 | async-start | bytes 25165824 | tf_op jit(solution)/shard_map/all_gather | solution.py:42
  132.5 0.7 copy-start.1
  132.5 1.8 copy-start.2
  132.5 197.7 %reduce-scatter.2.cloned.1.call-start = ((), (), s32[]{:S(2)}) async-start(), calls=%async_computation.4 | async-start | bytes 9437184 | tf_op jit(solution)/shard_map/reduce_scatter | solution.py:57
  135.9 2.2 copy-start
Sparse Core Ops, SparseCore 0:
  10.4 121.9 all-gather.2
  134.1 31.4 all-gather.4
  238.4 91.7 reduce-scatter.1

commit v2 on v1

v2 whole, which is shorter than its diff:
```python
import functools

import jax
import jax.numpy as jnp
from jax import lax
from jax.experimental import pallas as pl
from jax.experimental.pallas import tpu as pltpu
from jax.sharding import Mesh
from jax.sharding import PartitionSpec as P

BS = 128
BLK = ("blk_0", "blk_1", "blk_2")
GRP = ("grp_0", "grp_1")
TILE = 256


def expand_kernel(row_blocks, slots_ref, left_ref, right_ref, out_ref):
    step = pl.program_id(0)
    product = jnp.dot(left_ref[...], right_ref[...], preferred_element_type=jnp.float32)
    per_tile = TILE // BS
    for r in range(row_blocks):
        for t in range(per_tile):
            slot = slots_ref[r, step * per_tile + t]

            @pl.when(slot >= 0)
            def _():
                out_ref[pl.ds(r * BS, BS), pl.ds(pl.multiple_of(slot * BS, BS), BS)] = product[
                    r * BS:(r + 1) * BS, t * BS:(t + 1) * BS
                ]


def expand_packed(slots, left, right, half_blocks):
    rows, inner = left.shape
    width = right.shape[1]
    row_blocks = rows // BS
    return pl.pallas_call(
        functools.partial(expand_kernel, row_blocks),
        out_shape=jax.ShapeDtypeStruct((rows, half_blocks * BS), jnp.float32),
        grid_spec=pltpu.PrefetchScalarGridSpec(
            num_scalar_prefetch=1,
            grid=(width // TILE,),
            in_specs=[
                pl.BlockSpec((rows, inner), lambda i, s: (0, 0), pipeline_mode=pl.Buffered(1)),
                pl.BlockSpec((inner, TILE), lambda i, s: (0, i)),
            ],
            out_specs=pl.BlockSpec(
                (rows, half_blocks * BS), lambda i, s: (0, 0), pipeline_mode=pl.Buffered(1)
            ),
        ),
        compiler_params=pltpu.CompilerParams(
            dimension_semantics=("arbitrary",), vmem_limit_bytes=48 * 1024 * 1024
        ),
        cost_estimate=pl.CostEstimate(
            flops=2 * rows * inner * width,
            transcendentals=0,
            bytes_accessed=rows * inner * 2 + inner * width * 2 + rows * half_blocks * BS * 4,
        ),
    )(slots, left, right)


def shards(matrix, panels, pattern, pruned, owners):
    blk_count = lax.axis_size(BLK)
    blk_id = lax.axis_index(BLK)
    grp_id = lax.axis_index(GRP)
    row_count, inner = matrix.shape
    panel_width = panels.shape[1]
    row_blocks = row_count // BS
    inner_blocks = inner // BS
    panel_blocks = panel_width // BS
    width_total = panel_width * blk_count
    window_blocks = width_total // BS
    half_blocks = window_blocks // 2
    tile_left = lax.dynamic_slice(
        pattern, (blk_id * row_blocks, grp_id * inner_blocks), (row_blocks, inner_blocks)
    ).astype(jnp.bfloat16)
    left = (matrix.reshape(row_blocks, BS, inner_blocks, BS) * tile_left[:, None, :, None]).reshape(
        row_count, inner
    )
    tile_right = lax.dynamic_slice(
        pattern, (grp_id * inner_blocks, blk_id * panel_blocks), (inner_blocks, panel_blocks)
    ).astype(jnp.bfloat16)
    right = (
        panels.reshape(inner_blocks, BS, panel_blocks, BS) * tile_right[:, None, :, None]
    ).reshape(inner, panel_width)
    gathered = lax.all_gather(right, BLK, axis=1, tiled=True)
    local_pruned = lax.dynamic_slice_in_dim(pruned, blk_id * row_blocks, row_blocks, 0)
    local_slots = jnp.clip(jnp.cumsum(local_pruned, axis=1) - 1, 0, half_blocks - 1)
    slot_table = jnp.where(local_pruned > 0, local_slots, -1).astype(jnp.int32)
    packed = expand_packed(slot_table, left, gathered, half_blocks)
    summed_packed = lax.psum_scatter(packed, GRP, scatter_dimension=0, tiled=True)
    piece_rows = row_count // lax.axis_size(GRP)
    row_block = (blk_id * row_count + grp_id * piece_rows) // BS
    row_pruned = lax.dynamic_index_in_dim(pruned, row_block, 0, keepdims=False)
    slot_of = jnp.clip(jnp.cumsum(row_pruned) - 1, 0, half_blocks - 1)
    squared = summed_packed.reshape(piece_rows, half_blocks, BS)
    squared = squared * squared
    inverse = (
        jnp.zeros((window_blocks,), jnp.int32)
        .at[owners]
        .set(jnp.arange(window_blocks, dtype=jnp.int32))
    )
    picked = jnp.take(squared, slot_of[inverse], axis=1)
    kept = picked * row_pruned[inverse].astype(jnp.float32)[None, :, None]
    arranged = kept.reshape(1, piece_rows, width_total)
    moved = lax.all_to_all(arranged, BLK, split_axis=2, concat_axis=0, tiled=True)
    totals = lax.psum(jnp.sum(moved, axis=(0, 1)), GRP)
    normalized = (row_count * blk_count) * moved / totals
    return normalized[:, None, :, :]


def solution(mesh):
    split = Mesh(mesh.devices.reshape(2, 4, 2, 4, 2), ("grp_0", "grp_1", "blk_0", "blk_1", "blk_2"))
    placed = (P(BLK, GRP), P(GRP, BLK), P(), P(), P())
    return jax.shard_map(
        shards, mesh=split, in_specs=placed, out_specs=P(None, GRP, None, BLK), check_vma=False
    )
```

time: 449 us -> 358 us (0.80)
  blocking collectives: 99.7 us -> 54.4 us
  local copies, waits for them, and re-layouts: 54.5 us -> 13.7 us
  waiting for transfers between devices: 235 us -> 204 us
  Pallas kernels: 0 us -> 27.8 us
  matrix products: 23.6 us -> 0 us
  other arithmetic: 20.9 us -> 43.9 us
    psum x1, blocking collectives: 66.2 us -> 18.4 us  [shards(): totals = lax.psum(jnp.sum(moved, axis=(0, 1)), GRP)]
    reduce_sum x1 -> x2, other arithmetic: 1.35 us -> 30.5 us  [shards(): totals = lax.psum(jnp.sum(moved, axis=(0, 1)), GRP)]
    all_gather x2 -> x1, waiting for transfers between devices: 147 us -> 119 us  [shards(): gathered = lax.all_gather(right, BLK, axis=1, tiled=True)]
    pallas_call x0 -> x1, Pallas kernels: none -> 27.8 us  [expand_packed(): pl.pallas_call(functools.partial(expand_kernel, row_blocks), out_shape=ja...]
    dot_general x1 -> x0, matrix products: 23.6 us -> none  [shards(): partial_value = jnp.dot(left, gathered, preferred_element_type=jnp.float32)]
    dot_general x1 -> x0, local copies, waits for them, and re-layouts: 22.6 us -> none  [shards(): partial_value = jnp.dot(left, gathered, preferred_element_type=jnp.float32)]
    gather x8 -> x0, local copies, waits for them, and re-layouts: 12.8 us -> none  [the longest x2 10.2 us: shards(): jnp.take_along_axis(blocked, position[listing][:, None, :, None], axis=2)]
    select_n x3 -> x1, other arithmetic: 9.23 us -> 0.01 us  [shards(): slot_table = jnp.where(local_pruned > 0, local_slots, -1).astype(jnp.int32)]
  transfers between devices with their start and end apart: 3 -> 2, of which waited for: 3 -> 2; matrix products, arithmetic and copies ran while one was open for 2% -> 2% of each run, Pallas kernels for 0% -> 0%
where the time goes in v2:
time: 358 us; the launch traced here: 357 us
  waiting for transfers between devices  204 us (57%)
  blocking collectives  54.4 us (15%)
  other arithmetic  43.9 us (12%)
  Pallas kernels  27.8 us (8%)
  local copies, waits for them, and re-layouts  13.7 us (4%)
  between operations  13.5 us (4%)
    all_gather x1, waiting for transfers between devices, shards(): gathered = lax.all_gather(right, BLK, axis=1, tiled=True)  119 us
    reduce_scatter x1, waiting for transfers between devices, shards(): lax.psum_scatter(packed, GRP, scatter_dimension=0, tiled=True)  85.3 us
    all_to_all x1, blocking collectives, shards(): lax.all_to_all(arranged, BLK, split_axis=2, concat_axis=0, tiled=True)  36 us
    reduce_sum x2, other arithmetic, shards(): totals = lax.psum(jnp.sum(moved, axis=(0, 1)), GRP)  30.5 us
    pallas_call x1, Pallas kernels, expand_packed(): pl.pallas_call(functools.partial(expand_kernel, row_blocks), out_shape=ja...  27.8 us
    psum x1, blocking collectives, shards(): totals = lax.psum(jnp.sum(moved, axis=(0, 1)), GRP)  18.4 us
  transfers between devices with their start and end apart: 2, of which 2 were waited for; matrix products, arithmetic and copies ran while one was open for 2% of the time, Pallas kernels for 0%

profile of v2, /device:TPU:2, one launch (start us, length us, event | category | flops | bytes accessed | tf_op | source)
XLA Modules:
  0.0 357.4 jit_solution(8718076620673489990)
XLA Ops:
  6.5 0.8 dynamic-slice_convert_fusion
  7.3 0.6 mul.95
  7.9 2.4 bitcast_multiply_fusion.1
  10.7 0.8 dynamic-slice_convert_fusion.1
  11.5 0.6 mul.91
  12.1 1.6 copy-done.1
  13.7 2.8 bitcast_multiply_fusion.left_ref
  16.5 118.6 %all-gather.2.cloned.1.call-done.right_ref = bf16[2048,4096]{1,0:T(8,128)(2,1)} async-done(((bf16[2048,256]{1,0:T(8,128)(2,1)}), bf16[2048,4096]{1,0:T(8,128)(2,1)}) %all-gather.2.cloned.1.call-update) | async-done | bytes 16777232 | tf_op jit(solution)/shard_map/all_gather | solution.py:85
  135.2 2.2 copy-done
  137.4 27.8 %shard_map.55 = f32[1024,2048]{1,0:T(8,128)} custom-call(s32[8,32]{1,0:T(8,128)S(1)} %clamp_select_fusion.slots_ref, bf16[1024,2048]{1,0:T(8,128)(2,1)S(1)} %copy-done, bf16[2048,4096]{1,0:T(8,128)(2,1)} %all-gather.2.cloned.1.call-done.right_ref), custom_call_target="tpu_custom_call" | custom-call | flops 17179869184 | bytes 29360128 | tf_op jit(solution)/shard_map/pallas_call | solution.py:36
  165.8 0.7 scatter_custom_fusion
  166.6 0.7 gather_fusion
  167.4 0.7 gather_fusion.2
  168.4 85.3 %reduce-scatter.2.cloned.1.call-done = f32[128,2048]{1,0:T(8,128)} async-done(((f32[1024,2048]{1,0:T(8,128)}), f32[128,2048]{1,0:T(8,128)}) %reduce-scatter.2.cloned.1.call-update) | async-done | bytes 1048592 | tf_op jit(solution)/shard_map/reduce_scatter | solution.py:90
  253.7 1.3 copy_bitcast_fusion
  255.0 2.0 gather_fusion.1
  257.0 1.9 copy.42
  259.0 1.5 fusion
  260.5 36.0 %all_to_all.4 = f32[1,128,4096]{1,0,2:T(1,128)S(1)} all-to-all(f32[1,128,4096]{1,0,2:T(1,128)S(1)} %bitcast.33), channel_id=1, replica_groups=mesh['grp_0'=2,'grp_1'=4,'blk_0'=2,'blk_1'=4,'blk_2'=2] {'blk_0','blk_1'..., dimensions={2} | all-to-all | bytes 4194304 | tf_op jit(solution)/shard_map/all_to_all | solution.py:105
  296.5 1.5 broadcast_multiply_fusion
  297.9 30.5 %reduce_sum.10 = f32[4096]{0:T(1024)S(1)} reduce(f32[1,128,4096]{1,0,2:T(1,128)S(1)} %all_to_all.4, f32[]{:T(128)} %constant.84.clone.1), dimensions={0,1}, to_apply=%region_4.5 | reduce | flops 520192 | bytes 2113540 | tf_op jit(solution)/shard_map/reduce_sum | solution.py:106
  328.4 18.4 %psum.7 = f32[256]{0:T(256)S(1)} all-reduce(f32[256]{0:T(256)S(1)} %reduce_sum.18), channel_id=1, replica_groups=mesh['grp_0'=2,'grp_1'=4,'blk_0'=2,'blk_1'=4,'blk_2'=2] {'grp_0','grp_1'}, use_global_device_ids=true, to_apply=%region_6.7 | all-reduce | flops 256 | bytes 2048 | tf_op jit(solution)/shard_map/psum | solution.py:106
  346.9 1.9 divide_bitcast_fusion
  348.7 1.8 copy.45
  (30 shorter events, 1.5 us)
Async XLA Ops:
  6.5 128.6 %all-gather.2.cloned.1.call-start = ((), (), s32[]{:S(2)}) async-start(), calls=%async_computation.2 | async-start | bytes 17825792 | tf_op jit(solution)/shard_map/all_gather | solution.py:85
  7.9 2.5 copy-start.2
  10.3 243.4 %reduce-scatter.2.cloned.1.call-start = ((), (), s32[]{:S(2)}) async-start(), calls=%async_computation.3 | async-start | bytes 9437184 | tf_op jit(solution)/shard_map/reduce_scatter | solution.py:90
  11.5 2.2 copy-start.1
  135.2 2.2 copy-start
  165.2 0.7 copy-start.3
Sparse Core Ops, SparseCore 0:
  10.5 124.6 all-gather.1
  165.3 88.3 reduce-scatter.1

commit v3 on v2

--- a/solution.py
+++ b/solution.py
@@ -101,10 +101,12 @@
     )
     picked = jnp.take(squared, slot_of[inverse], axis=1)
     kept = picked * row_pruned[inverse].astype(jnp.float32)[None, :, None]
-    arranged = kept.reshape(1, piece_rows, width_total)
-    moved = lax.all_to_all(arranged, BLK, split_axis=2, concat_axis=0, tiled=True)
-    totals = lax.psum(jnp.sum(moved, axis=(0, 1)), GRP)
-    normalized = (row_count * blk_count) * moved / totals
+    arranged = kept.reshape(piece_rows, width_total)
+    sums = jnp.zeros((8, width_total), jnp.float32).at[0].set(jnp.sum(arranged, axis=0))
+    payload = jnp.concatenate([arranged, sums], axis=0)[None]
+    moved = lax.all_to_all(payload, BLK, split_axis=2, concat_axis=0, tiled=True)
+    totals = lax.psum(jnp.sum(moved[:, piece_rows, :], axis=0), GRP)
+    normalized = (row_count * blk_count) * moved[:, :piece_rows, :] / totals
     return normalized[:, None, :, :]
 
 

time: 358 us -> 376 us (1.050)
  other arithmetic: 43.9 us -> 11.2 us
  local copies, waits for them, and re-layouts: 13.7 us -> 42 us
  blocking collectives: 54.4 us -> 77 us
    reduce_sum x2, other arithmetic: 30.5 us -> 0.5 us  [the longest x1 0.48 us: shards(): jnp.sum(arranged, axis=0)]
    all_to_all x1, blocking collectives: 36 us -> 58.5 us  [shards(): lax.all_to_all(payload, BLK, split_axis=2, concat_axis=0, tiled=True)]
    broadcast_in_dim x0 -> x2, local copies, waits for them, and re-layouts: none -> 19.5 us  [the longest x1 17 us: shards(): payload = jnp.concatenate([arranged, sums], axis=0)[None]]
    all_to_all x0 -> x2, local copies, waits for them, and re-layouts: none -> 9.18 us  [shards(): lax.all_to_all(payload, BLK, split_axis=2, concat_axis=0, tiled=True)]
where the time goes in v3:
time: 376 us
  waiting for transfers between devices  204 us (54%)
  blocking collectives  77 us (20%)
  local copies, waits for them, and re-layouts  42 us (11%)
  Pallas kernels  27.8 us (7%)
  between operations  13.6 us (4%)
  other arithmetic  11.2 us (3%)
    all_gather x1, waiting for transfers between devices, shards(): gathered = lax.all_gather(right, BLK, axis=1, tiled=True)  119 us
    reduce_scatter x1, waiting for transfers between devices, shards(): lax.psum_scatter(packed, GRP, scatter_dimension=0, tiled=True)  85.3 us
    all_to_all x1, blocking collectives, shards(): lax.all_to_all(payload, BLK, split_axis=2, concat_axis=0, tiled=True)  58.5 us
    pallas_call x1, Pallas kernels, expand_packed(): pl.pallas_call(functools.partial(expand_kernel, row_blocks), out_shape=ja...  27.8 us
    psum x1, blocking collectives, shards(): totals = lax.psum(jnp.sum(moved[:, piece_rows, :], axis=0), GRP)  18.4 us
    broadcast_in_dim x1, local copies, waits for them, and re-layouts, shards(): payload = jnp.concatenate([arranged, sums], axis=0)[None]  17 us
    all_to_all x2, local copies, waits for them, and re-layouts, shards(): lax.all_to_all(payload, BLK, split_axis=2, concat_axis=0, tiled=True)  9.18 us
  transfers between devices with their start and end apart: 2, of which 2 were waited for; matrix products, arithmetic and copies ran while one was open for 2% of the time, Pallas kernels for 0%

profile of v3, /device:TPU:2, one launch (start us, length us, event | category | flops | bytes accessed | tf_op | source)
XLA Modules:
  0.0 375.5 jit_solution(1111006671457026769)
XLA Ops:
  6.5 0.8 dynamic-slice_convert_fusion
  7.3 0.6 mul.89
  7.9 2.4 bitcast_multiply_fusion.1
  10.7 0.8 dynamic-slice_convert_fusion.1
  12.1 1.6 copy-done.3
  13.7 2.8 bitcast_multiply_fusion.left_ref
  16.5 118.6 %all-gather.2.cloned.1.call-done.right_ref = bf16[2048,4096]{1,0:T(8,128)(2,1)} async-done(((bf16[2048,256]{1,0:T(8,128)(2,1)}), bf16[2048,4096]{1,0:T(8,128)(2,1)}) %all-gather.2.cloned.1.call-update) | async-done | bytes 16777232 | tf_op jit(solution)/shard_map/all_gather | solution.py:85
  135.2 2.2 copy-done
  137.4 27.8 %shard_map.55 = f32[1024,2048]{1,0:T(8,128)} custom-call(s32[8,32]{1,0:T(8,128)S(1)} %clamp_select_fusion.slots_ref, bf16[1024,2048]{1,0:T(8,128)(2,1)S(1)} %copy-done, bf16[2048,4096]{1,0:T(8,128)(2,1)} %all-gather.2.cloned.1.call-done.right_ref), custom_call_target="tpu_custom_call" | custom-call | flops 17179869184 | bytes 29360128 | tf_op jit(solution)/shard_map/pallas_call | solution.py:36
  165.8 0.7 scatter_custom_fusion
  166.6 0.7 gather_fusion
  167.4 0.7 gather_fusion.2
  168.4 85.3 %reduce-scatter.2.cloned.1.call-done = f32[128,2048]{1,0:T(8,128)} async-done(((f32[1024,2048]{1,0:T(8,128)}), f32[128,2048]{1,0:T(8,128)}) %reduce-scatter.2.cloned.1.call-update) | async-done | bytes 1048592 | tf_op jit(solution)/shard_map/reduce_scatter | solution.py:90
  253.7 1.3 copy_bitcast_fusion
  255.0 0.7 gather_fusion.1
  256.2 1.9 copy.43
  258.1 2.0 copy.44
  260.1 1.5 fusion.3
  262.0 17.0 %copy.45 = f32[1,136,4096]{1,0,2:T(1,128)S(1)} copy(f32[1,136,4096]{1,2,0:T(8,128)S(1)} %fusion) | data formatting | bytes 4456448 | tf_op jit(solution)/shard_map/broadcast_in_dim | solution.py:106
  278.9 58.5 %all_to_all.18 = f32[1,136,4096]{1,0,2:T(1,128)} all-to-all(f32[1,136,4096]{1,0,2:T(1,128)S(1)} %copy.45), channel_id=1, replica_groups=mesh['grp_0'=2,'grp_1'=4,'blk_0'=2,'blk_1'=4,'blk_2'=2] {'blk_0','blk_1'..., dimensions={2} | all-to-all | bytes 4456448 | tf_op jit(solution)/shard_map/all_to_all | solution.py:107
  337.5 9.0 %copy.46 = f32[1,136,4096]{2,1,0:T(8,128)S(1)} copy(f32[1,136,4096]{1,0,2:T(1,128)} %all_to_all.18) | data formatting | bytes 4456448 | tf_op jit(solution)/shard_map/all_to_all | solution.py:107
  346.5 0.7 copy.52
  347.4 18.4 %psum.7 = f32[256]{0:T(256)S(1)} all-reduce(f32[256]{0:T(256)S(1)} %slice_reduce_fusion), channel_id=1, replica_groups=mesh['grp_0'=2,'grp_1'=4,'blk_0'=2,'blk_1'=4,'blk_2'=2] {'grp_0','grp_1'}, use_global_device_ids=true, to_apply=%region_6.7 | all-reduce | flops 256 | bytes 2048 | tf_op jit(solution)/shard_map/psum | solution.py:108
  366.1 2.5 copy.47
  (38 shorter events, 3.4 us)
Async XLA Ops:
  6.5 128.6 %all-gather.2.cloned.1.call-start = ((), (), s32[]{:S(2)}) async-start(), calls=%async_computation.2 | async-start | bytes 17825792 | tf_op jit(solution)/shard_map/all_gather | solution.py:85
  7.9 2.5 copy-start.4
  10.3 243.4 %reduce-scatter.2.cloned.1.call-start = ((), (), s32[]{:S(2)}) async-start(), calls=%async_computation.3 | async-start | bytes 9437184 | tf_op jit(solution)/shard_map/reduce_scatter | solution.py:90
  11.5 2.2 copy-start.3
  135.2 2.2 copy-start
  165.2 0.7 copy-start.5
  258.1 2.0 copy-start.1
  260.1 1.6 copy-start.2
Sparse Core Ops, SparseCore 0:
  10.5 124.6 all-gather.1
  165.3 88.3 reduce-scatter.1

commit v4 on v2

--- a/solution.py
+++ b/solution.py
@@ -101,8 +101,12 @@
     )
     picked = jnp.take(squared, slot_of[inverse], axis=1)
     kept = picked * row_pruned[inverse].astype(jnp.float32)[None, :, None]
-    arranged = kept.reshape(1, piece_rows, width_total)
-    moved = lax.all_to_all(arranged, BLK, split_axis=2, concat_axis=0, tiled=True)
+    arranged = (
+        kept.reshape(piece_rows, blk_count, window_blocks // blk_count, BS)
+        .transpose(1, 0, 2, 3)
+        .reshape(blk_count, piece_rows, panel_width)
+    )
+    moved = lax.all_to_all(arranged, BLK, split_axis=0, concat_axis=0, tiled=True)
     totals = lax.psum(jnp.sum(moved, axis=(0, 1)), GRP)
     normalized = (row_count * blk_count) * moved / totals
     return normalized[:, None, :, :]

time: 358 us -> 320 us (0.89)
  other arithmetic: 43.9 us -> 10.8 us
  local copies, waits for them, and re-layouts: 13.7 us -> 8.7 us
    reduce_sum x2 -> x1, other arithmetic: 30.5 us -> 0.28 us  [shards(): totals = lax.psum(jnp.sum(moved, axis=(0, 1)), GRP)]
where the time goes in v4:
time: 320 us; the launch traced here: 319 us
  waiting for transfers between devices  204 us (64%)
  blocking collectives  54.4 us (17%)
  Pallas kernels  27.8 us (9%)
  between operations  13.5 us (4%)
  other arithmetic  10.8 us (3%)
  local copies, waits for them, and re-layouts  8.7 us (3%)
    all_gather x1, waiting for transfers between devices, shards(): gathered = lax.all_gather(right, BLK, axis=1, tiled=True)  119 us
    reduce_scatter x1, waiting for transfers between devices, shards(): lax.psum_scatter(packed, GRP, scatter_dimension=0, tiled=True)  85.2 us
    all_to_all x1, blocking collectives, shards(): lax.all_to_all(arranged, BLK, split_axis=0, concat_axis=0, tiled=True)  36 us
    pallas_call x1, Pallas kernels, expand_packed(): pl.pallas_call(functools.partial(expand_kernel, row_blocks), out_shape=ja...  27.8 us
    psum x1, blocking collectives, shards(): totals = lax.psum(jnp.sum(moved, axis=(0, 1)), GRP)  18.4 us
  transfers between devices with their start and end apart: 2, of which 2 were waited for; matrix products, arithmetic and copies ran while one was open for 2% of the time, Pallas kernels for 0%

profile of v4, /device:TPU:2, one launch (start us, length us, event | category | flops | bytes accessed | tf_op | source)
XLA Modules:
  0.0 319.1 jit_solution(6165208584008407099)
XLA Ops:
  6.5 0.8 dynamic-slice_convert_fusion
  7.3 0.6 mul.80
  7.9 2.4 bitcast_multiply_fusion.1
  10.5 0.2 reduce_window_sum.18
  10.7 0.8 dynamic-slice_convert_fusion.1
  11.5 0.6 mul.76
  12.1 1.6 copy-done.1
  13.7 2.8 bitcast_multiply_fusion.left_ref
  16.5 118.6 %all-gather.2.cloned.1.call-done.right_ref = bf16[2048,4096]{1,0:T(8,128)(2,1)} async-done(((bf16[2048,256]{1,0:T(8,128)(2,1)}), bf16[2048,4096]{1,0:T(8,128)(2,1)}) %all-gather.2.cloned.1.call-update) | async-done | bytes 16777232 | tf_op jit(solution)/shard_map/all_gather | solution.py:85
  135.2 2.2 copy-done
  137.4 27.8 %shard_map.55 = f32[1024,2048]{1,0:T(8,128)} custom-call(s32[8,32]{1,0:T(8,128)S(1)} %clamp_select_fusion.slots_ref, bf16[1024,2048]{1,0:T(8,128)(2,1)S(1)} %copy-done, bf16[2048,4096]{1,0:T(8,128)(2,1)} %all-gather.2.cloned.1.call-done.right_ref), custom_call_target="tpu_custom_call" | custom-call | flops 17179869184 | bytes 29360128 | tf_op jit(solution)/shard_map/pallas_call | solution.py:36
  165.2 0.2 dynamic-slice_reduce_fusion
  165.4 0.4 copy-done.3
  165.8 0.7 scatter_custom_fusion
  166.6 0.7 gather_fusion
  167.5 0.7 gather_fusion.2
  168.5 85.2 %reduce-scatter.2.cloned.1.call-done = f32[128,2048]{1,0:T(8,128)} async-done(((f32[1024,2048]{1,0:T(8,128)}), f32[128,2048]{1,0:T(8,128)}) %reduce-scatter.2.cloned.1.call-update) | async-done | bytes 1048592 | tf_op jit(solution)/shard_map/reduce_scatter | solution.py:90
  253.7 1.3 copy_bitcast_fusion.1
  255.0 0.7 gather_fusion.1
  255.7 0.3 copy_bitcast_fusion
  256.0 36.0 %all_to_all.5 = f32[16,128,256]{2,1,0:T(8,128)S(1)} all-to-all(f32[16,128,256]{2,1,0:T(8,128)S(1)} %copy_bitcast_fusion), channel_id=1, replica_groups=mesh['grp_0'=2,'grp_1'=4,'blk_0'=2,'blk_1'=4,'blk_2'=2] {'blk_0','blk_1'..., dimensions={0} | all-to-all | bytes 4194304 | tf_op jit(solution)/shard_map/all_to_all | solution.py:109
  292.0 0.3 reduce_sum.9
  292.3 18.4 %psum.7 = f32[256]{0:T(256)S(1)} all-reduce(f32[256]{0:T(256)S(1)} %reduce_sum.9), channel_id=1, replica_groups=mesh['grp_0'=2,'grp_1'=4,'blk_0'=2,'blk_1'=4,'blk_2'=2] {'grp_0','grp_1'}, use_global_device_ids=true, to_apply=%region_5.6 | all-reduce | flops 256 | bytes 2048 | tf_op jit(solution)/shard_map/psum | solution.py:110
  310.7 1.6 divide_bitcast_fusion
  (25 shorter events, 0.8 us)
Async XLA Ops:
  6.5 128.6 %all-gather.2.cloned.1.call-start = ((), (), s32[]{:S(2)}) async-start(), calls=%async_computation.2 | async-start | bytes 17825792 | tf_op jit(solution)/shard_map/all_gather | solution.py:85
  7.9 2.5 copy-start.2
  10.3 243.4 %reduce-scatter.2.cloned.1.call-start = ((), (), s32[]{:S(2)}) async-start(), calls=%async_computation.3 | async-start | bytes 9437184 | tf_op jit(solution)/shard_map/reduce_scatter | solution.py:90
  11.5 2.2 copy-start.1
  135.2 2.2 copy-start
  165.2 0.7 copy-start.3
Sparse Core Ops, SparseCore 0:
  10.5 124.6 all-gather.1
  165.3 88.3 reduce-scatter.1

commit v5 on v2

--- a/solution.py
+++ b/solution.py
@@ -14,7 +14,7 @@
 TILE = 256
 
 
-def expand_kernel(row_blocks, slots_ref, left_ref, right_ref, out_ref):
+def expand_kernel(row_blocks, height, slots_ref, left_ref, right_ref, out_ref):
     step = pl.program_id(0)
     product = jnp.dot(left_ref[...], right_ref[...], preferred_element_type=jnp.float32)
     per_tile = TILE // BS
@@ -24,17 +24,17 @@
 
             @pl.when(slot >= 0)
             def _():
-                out_ref[pl.ds(r * BS, BS), pl.ds(pl.multiple_of(slot * BS, BS), BS)] = product[
-                    r * BS:(r + 1) * BS, t * BS:(t + 1) * BS
+                out_ref[pl.ds(r * height, height), pl.ds(pl.multiple_of(slot * BS, BS), BS)] = product[
+                    r * height:(r + 1) * height, t * BS:(t + 1) * BS
                 ]
 
 
 def expand_packed(slots, left, right, half_blocks):
     rows, inner = left.shape
     width = right.shape[1]
-    row_blocks = rows // BS
+    row_blocks = slots.shape[0]
     return pl.pallas_call(
-        functools.partial(expand_kernel, row_blocks),
+        functools.partial(expand_kernel, row_blocks, rows // row_blocks),
         out_shape=jax.ShapeDtypeStruct((rows, half_blocks * BS), jnp.float32),
         grid_spec=pltpu.PrefetchScalarGridSpec(
             num_scalar_prefetch=1,
@@ -86,24 +86,46 @@
     local_pruned = lax.dynamic_slice_in_dim(pruned, blk_id * row_blocks, row_blocks, 0)
     local_slots = jnp.clip(jnp.cumsum(local_pruned, axis=1) - 1, 0, half_blocks - 1)
     slot_table = jnp.where(local_pruned > 0, local_slots, -1).astype(jnp.int32)
-    packed = expand_packed(slot_table, left, gathered, half_blocks)
-    summed_packed = lax.psum_scatter(packed, GRP, scatter_dimension=0, tiled=True)
     piece_rows = row_count // lax.axis_size(GRP)
     row_block = (blk_id * row_count + grp_id * piece_rows) // BS
     row_pruned = lax.dynamic_index_in_dim(pruned, row_block, 0, keepdims=False)
     slot_of = jnp.clip(jnp.cumsum(row_pruned) - 1, 0, half_blocks - 1)
-    squared = summed_packed.reshape(piece_rows, half_blocks, BS)
-    squared = squared * squared
     inverse = (
         jnp.zeros((window_blocks,), jnp.int32)
         .at[owners]
         .set(jnp.arange(window_blocks, dtype=jnp.int32))
     )
-    picked = jnp.take(squared, slot_of[inverse], axis=1)
-    kept = picked * row_pruned[inverse].astype(jnp.float32)[None, :, None]
-    arranged = kept.reshape(1, piece_rows, width_total)
-    moved = lax.all_to_all(arranged, BLK, split_axis=2, concat_axis=0, tiled=True)
-    totals = lax.psum(jnp.sum(moved, axis=(0, 1)), GRP)
+    halves = 2
+    half_rows = piece_rows // halves
+    split_left = left.reshape(row_blocks, halves, BS // halves, inner)
+    def expand(h):
+        part_left = split_left[:, h].reshape(row_count // halves, inner)
+        return expand_packed(slot_table, part_left, gathered, half_blocks)
+
+    def arrange(summed_packed):
+        squared = summed_packed.reshape(half_rows, half_blocks, BS)
+        squared = squared * squared
+        picked = jnp.take(squared, slot_of[inverse], axis=1)
+        kept = picked * row_pruned[inverse].astype(jnp.float32)[None, :, None]
+        return (
+            kept.reshape(half_rows, blk_count, window_blocks // blk_count, BS)
+            .transpose(1, 0, 2, 3)
+            .reshape(blk_count, half_rows, panel_width)
+        )
+
+    moved_parts = []
+    packed = expand(0)
+    for h in range(halves):
+        summed_packed = lax.psum_scatter(packed, GRP, scatter_dimension=0, tiled=True)
+        if h + 1 < halves:
+            packed = expand(h + 1)
+        arranged = arrange(summed_packed)
+        if h + 1 < halves:
+            arranged, packed = lax.optimization_barrier((arranged, packed))
+        moved_parts.append(lax.all_to_all(arranged, BLK, split_axis=0, concat_axis=0, tiled=True))
+    moved = jnp.concatenate(moved_parts, axis=1)
+    local_sums = sum(jnp.sum(part, axis=(0, 1)) for part in moved_parts)
+    totals = lax.psum(local_sums, GRP)
     normalized = (row_count * blk_count) * moved / totals
     return normalized[:, None, :, :]
 

time: 358 us -> 325 us (0.908)
  blocking collectives: 54.4 us -> 18.7 us
  other arithmetic: 43.9 us -> 11.2 us
  Pallas kernels: 27.8 us -> 41.3 us
  starting transfers between devices: 0.04 us -> 13.4 us
  waiting for transfers between devices: 204 us -> 215 us
    all_to_all x1 -> x0, blocking collectives: 36 us -> none  [shards(): lax.all_to_all(arranged, BLK, split_axis=2, concat_axis=0, tiled=True)]
    reduce_sum x2, other arithmetic: 30.5 us -> 0.3 us  [shards(): local_sums = sum((jnp.sum(part, axis=(0, 1)) for part in moved_parts))]
    all_to_all x0 -> x2, waiting for transfers between devices: none -> 17.8 us  [shards(): lax.all_to_all(arranged, BLK, split_axis=0, concat_axis=0, tiled=True)]
    pallas_call x1 -> x2, Pallas kernels: 27.8 us -> 41.3 us  [expand_packed(): pl.pallas_call(functools.partial(expand_kernel, row_blocks, rows // row_b...]
    all_to_all x0 -> x2, starting transfers between devices: none -> 13.3 us  [shards(): lax.all_to_all(arranged, BLK, split_axis=0, concat_axis=0, tiled=True)]
    reduce_scatter x1 -> x2, waiting for transfers between devices: 85.3 us -> 78 us  [shards(): lax.psum_scatter(packed, GRP, scatter_dimension=0, tiled=True)]
  transfers between devices with their start and end apart: 2 -> 5, of which waited for: 2 -> 4; matrix products, arithmetic and copies ran while one was open for 2% -> 3% of each run, Pallas kernels for 0% -> 6%
where the time goes in v5:
time: 325 us; the launch traced here: 323 us
  waiting for transfers between devices  215 us (66%)
  Pallas kernels  41.3 us (13%)
  blocking collectives  18.7 us (6%)
  starting transfers between devices  13.4 us (4%)
  between operations  13.3 us (4%)
  other arithmetic  11.2 us (3%)
  local copies, waits for them, and re-layouts  10.2 us (3%)
    all_gather x1, waiting for transfers between devices, shards(): gathered = lax.all_gather(right, BLK, axis=1, tiled=True)  119 us
    reduce_scatter x2, waiting for transfers between devices, shards(): lax.psum_scatter(packed, GRP, scatter_dimension=0, tiled=True)  78 us
    pallas_call x2, Pallas kernels, expand_packed(): pl.pallas_call(functools.partial(expand_kernel, row_blocks, rows // row_b...  41.3 us
    psum x1, blocking collectives, shards(): totals = lax.psum(local_sums, GRP)  18.7 us
    all_to_all x2, waiting for transfers between devices, shards(): lax.all_to_all(arranged, BLK, split_axis=0, concat_axis=0, tiled=True)  17.8 us
    all_to_all x2, starting transfers between devices, shards(): lax.all_to_all(arranged, BLK, split_axis=0, concat_axis=0, tiled=True)  13.3 us
  transfers between devices with their start and end apart: 5, of which 4 were waited for; matrix products, arithmetic and copies ran while one was open for 3% of the time, Pallas kernels for 6%

profile of v5, /device:TPU:2, one launch (start us, length us, event | category | flops | bytes accessed | tf_op | source)
XLA Modules:
  0.0 323.2 jit_solution(16625918561124213689)
XLA Ops:
  6.5 0.8 dynamic-slice_convert_fusion
  7.9 2.4 bitcast_multiply_fusion
  10.8 0.8 dynamic-slice_convert_fusion.1
  11.7 2.5 copy_multiply_fusion
  14.2 1.7 fusion.3
  15.9 119.3 %all-gather.2.cloned.1.call-done.right_ref = bf16[2048,4096]{1,0:T(8,128)(2,1)} async-done(((bf16[2048,256]{1,0:T(8,128)(2,1)}), bf16[2048,4096]{1,0:T(8,128)(2,1)}) %all-gather.2.cloned.1.call-update) | async-done | bytes 16777232 | tf_op jit(solution)/shard_map/all_gather | solution.py:85
  135.2 1.6 copy-done
  136.8 20.6 %shard_map.55 = f32[512,2048]{1,0:T(8,128)} custom-call(s32[8,32]{1,0:T(8,128)S(1)} %clamp_select_fusion.slots_ref, bf16[512,2048]{1,0:T(8,128)(2,1)S(1)} %bitcast.42, bf16[2048,4096]{1,0:T(8,128)(2,1)} %all-gather.2.cloned.1.call-done.right_ref), custom_call_target="tpu_custom_call" | custom-call | flops 8589934592 | bytes 23068672 | tf_op jit(solution)/shard_map/pallas_call | solution.py:36
  158.0 0.7 scatter_custom_fusion
  158.8 0.7 gather_fusion
  159.5 0.7 gather_fusion.1
  160.3 20.7 %shard_map.56 = f32[512,2048]{1,0:T(8,128)} custom-call(s32[8,32]{1,0:T(8,128)S(1)} %clamp_select_fusion.slots_ref, bf16[512,2048]{1,0:T(8,128)(2,1)S(1)} %bitcast.41, bf16[2048,4096]{1,0:T(8,128)(2,1)} %all-gather.2.cloned.1.call-done.right_ref), custom_call_target="tpu_custom_call" | custom-call | flops 8589934592 | bytes 23068672 | tf_op jit(solution)/shard_map/pallas_call | solution.py:36
  181.0 25.4 %reduce-scatter.3.cloned.1.call-done = f32[64,2048]{1,0:T(8,128)} async-done(((f32[512,2048]{1,0:T(8,128)}), f32[64,2048]{1,0:T(8,128)}) %reduce-scatter.3.cloned.1.call-update) | async-done | bytes 524304 | tf_op jit(solution)/shard_map/reduce_scatter | solution.py:119
  206.4 1.1 copy_bitcast_fusion.3
  207.5 0.6 gather_fusion.2
  208.3 1.1 copy.33
  209.4 6.9 %all-to-all-start = ((f32[16,64,256]{2,1,0:T(8,128)}), f32[16,64,256]{2,1,0:T(8,128)S(1)}, u32[]{:S(2)}, u32[]{:S(2)}) async-start(f32[16,64,256]{2,1,0:T(8,128)} %bitcast.40), calls=%async_computation.1 | async-start | bytes 2097152 | tf_op jit(solution)/shard_map/all_to_all | solution.py:125
  216.3 52.6 %reduce-scatter.5.cloned.1.call-done = f32[64,2048]{1,0:T(8,128)} async-done(((f32[512,2048]{1,0:T(8,128)}), f32[64,2048]{1,0:T(8,128)}) %reduce-scatter.5.cloned.1.call-update) | async-done | bytes 524304 | tf_op jit(solution)/shard_map/reduce_scatter | solution.py:119
  268.9 1.1 copy_bitcast_fusion.2
  270.8 1.1 copy.32
  271.9 6.5 %all-to-all-start.1 = ((f32[16,64,256]{2,1,0:T(8,128)}), f32[16,64,256]{2,1,0:T(8,128)S(1)}, u32[]{:S(2)}, u32[]{:S(2)}) async-start(f32[16,64,256]{2,1,0:T(8,128)} %bitcast.39), calls=%async_computation.3 | async-start | bytes 2097152 | tf_op jit(solution)/shard_map/all_to_all | solution.py:125
  278.5 17.8 %all-to-all-done.1 = f32[16,64,256]{2,1,0:T(8,128)S(1)} async-done(((f32[16,64,256]{2,1,0:T(8,128)}), f32[16,64,256]{2,1,0:T(8,128)S(1)}, u32[]{:S(2)}, u32[]{:S(2)}) %all-to-all-start.1) | async-done | bytes 1048608 | tf_op jit(solution)/shard_map/all_to_all | solution.py:125
  296.4 18.7 %psum.7 = f32[256]{0:T(256)S(1)} all-reduce(f32[256]{0:T(256)S(1)} %add.65), channel_id=1, replica_groups=mesh['grp_0'=2,'grp_1'=4,'blk_0'=2,'blk_1'=4,'blk_2'=2] {'grp_0','grp_1'}, use_global_device_ids=true, to_apply=%region_7.9 | all-reduce | flops 256 | bytes 2048 | tf_op jit(solution)/shard_map/psum | solution.py:128
  315.1 1.6 fusion
  (36 shorter events, 3.2 us)
Async XLA Ops:
  6.5 128.7 %all-gather.2.cloned.1.call-start = ((), (), s32[]{:S(2)}) async-start(), calls=%async_computation.4 | async-start | bytes 17825792 | tf_op jit(solution)/shard_map/all_gather | solution.py:85
  7.9 2.5 copy-start.1
  10.4 196.1 %reduce-scatter.3.cloned.1.call-start = ((), (), s32[]{:S(2)}) async-start(), calls=%async_computation.5 | async-start | bytes 4718592 | tf_op jit(solution)/shard_map/reduce_scatter | solution.py:119
  135.2 1.6 copy-start
  157.4 0.7 copy-start.2
  157.4 111.5 %reduce-scatter.5.cloned.1.call-start = ((), (), s32[]{:S(2)}) async-start(), calls=%async_computation.6 | async-start | bytes 4718592 | tf_op jit(solution)/shard_map/reduce_scatter | solution.py:119
  209.4 62.4 %all-to-all-start = ((f32[16,64,256]{2,1,0:T(8,128)}), f32[16,64,256]{2,1,0:T(8,128)S(1)}, u32[]{:S(2)}, u32[]{:S(2)}) async-start(f32[16,64,256]{2,1,0:T(8,128)} %bitcast.40), calls=%async_computation.1 | async-start | bytes 2097152 | tf_op jit(solution)/shard_map/all_to_all | solution.py:125
  271.9 24.4 %all-to-all-start.1 = ((f32[16,64,256]{2,1,0:T(8,128)}), f32[16,64,256]{2,1,0:T(8,128)S(1)}, u32[]{:S(2)}, u32[]{:S(2)}) async-start(f32[16,64,256]{2,1,0:T(8,128)} %bitcast.39), calls=%async_computation.3 | async-start | bytes 2097152 | tf_op jit(solution)/shard_map/all_to_all | solution.py:125
Sparse Core Ops, SparseCore 0:
  10.5 124.6 all-gather.1
  157.5 48.8 reduce-scatter.2
  209.6 59.2 reduce-scatter.4

commit v6 on v4

--- a/solution.py
+++ b/solution.py
@@ -107,7 +107,10 @@
         .reshape(blk_count, piece_rows, panel_width)
     )
     moved = lax.all_to_all(arranged, BLK, split_axis=0, concat_axis=0, tiled=True)
-    totals = lax.psum(jnp.sum(moved, axis=(0, 1)), GRP)
+    group_sums = lax.psum(jnp.sum(arranged, axis=1), GRP)
+    group_sums, moved = lax.optimization_barrier((group_sums, moved))
+    owner_sums = lax.all_to_all(group_sums, BLK, split_axis=0, concat_axis=0, tiled=True)
+    totals = jnp.sum(owner_sums, axis=0)
     normalized = (row_count * blk_count) * moved / totals
     return normalized[:, None, :, :]
 

time: 320 us -> 326 us (1.019)
  blocking collectives: 54.4 us -> 47.1 us
  starting transfers between devices: 0.04 us -> 7.07 us
    all_to_all x1, blocking collectives: 36 us -> 14.8 us  [shards(): lax.all_to_all(group_sums, BLK, split_axis=0, concat_axis=0, tiled=True)]
    psum x1, blocking collectives: 18.4 us -> 32.2 us  [shards(): group_sums = lax.psum(jnp.sum(arranged, axis=1), GRP)]
    all_to_all x0 -> x1, starting transfers between devices: none -> 7.02 us  [shards(): lax.all_to_all(arranged, BLK, split_axis=0, concat_axis=0, tiled=True)]
  transfers between devices with their start and end apart: 2 -> 3, of which waited for: 2 -> 2; matrix products, arithmetic and copies ran while one was open for 2% -> 2% of each run, Pallas kernels for 0% -> 0%
where the time goes in v6:
time: 326 us; the launch traced here: 322 us
  waiting for transfers between devices  204 us (63%)
  blocking collectives  47.1 us (14%)
  Pallas kernels  27.8 us (9%)
  other arithmetic  13.8 us (4%)
  between operations  13.6 us (4%)
  local copies, waits for them, and re-layouts  8.72 us (3%)
  starting transfers between devices  7.07 us (2%)
    all_gather x1, waiting for transfers between devices, shards(): gathered = lax.all_gather(right, BLK, axis=1, tiled=True)  119 us
    reduce_scatter x1, waiting for transfers between devices, shards(): lax.psum_scatter(packed, GRP, scatter_dimension=0, tiled=True)  85.2 us
    psum x1, blocking collectives, shards(): group_sums = lax.psum(jnp.sum(arranged, axis=1), GRP)  32.2 us
    pallas_call x1, Pallas kernels, expand_packed(): pl.pallas_call(functools.partial(expand_kernel, row_blocks), out_shape=ja...  27.8 us
    all_to_all x1, blocking collectives, shards(): lax.all_to_all(group_sums, BLK, split_axis=0, concat_axis=0, tiled=True)  14.8 us
    all_to_all x1, starting transfers between devices, shards(): lax.all_to_all(arranged, BLK, split_axis=0, concat_axis=0, tiled=True)  7.02 us
  transfers between devices with their start and end apart: 3, of which 2 were waited for; matrix products, arithmetic and copies ran while one was open for 2% of the time, Pallas kernels for 0%

profile of v6, /device:TPU:2, one launch (start us, length us, event | category | flops | bytes accessed | tf_op | source)
XLA Modules:
  0.0 321.9 jit_solution(12877345021367278593)
XLA Ops:
  6.5 0.8 dynamic-slice_convert_fusion
  7.3 0.6 mul.80
  7.9 2.4 bitcast_multiply_fusion.1
  10.5 0.2 reduce_window_sum.18
  10.7 0.8 dynamic-slice_convert_fusion.1
  11.5 0.6 mul.76
  12.1 1.6 copy-done.1
  13.7 2.8 bitcast_multiply_fusion.left_ref
  16.5 118.6 %all-gather.2.cloned.1.call-done.right_ref = bf16[2048,4096]{1,0:T(8,128)(2,1)} async-done(((bf16[2048,256]{1,0:T(8,128)(2,1)}), bf16[2048,4096]{1,0:T(8,128)(2,1)}) %all-gather.2.cloned.1.call-update) | async-done | bytes 16777232 | tf_op jit(solution)/shard_map/all_gather | solution.py:85
  135.2 2.2 copy-done
  137.4 27.8 %shard_map.55 = f32[1024,2048]{1,0:T(8,128)} custom-call(s32[8,32]{1,0:T(8,128)S(1)} %clamp_select_fusion.slots_ref, bf16[1024,2048]{1,0:T(8,128)(2,1)S(1)} %copy-done, bf16[2048,4096]{1,0:T(8,128)(2,1)} %all-gather.2.cloned.1.call-done.right_ref), custom_call_target="tpu_custom_call" | custom-call | flops 17179869184 | bytes 29360128 | tf_op jit(solution)/shard_map/pallas_call | solution.py:36
  165.4 0.4 copy-done.3
  165.8 0.7 scatter_custom_fusion
  166.6 0.7 gather_fusion
  167.5 0.7 gather_fusion.2
  168.5 85.2 %reduce-scatter.2.cloned.1.call-done = f32[128,2048]{1,0:T(8,128)} async-done(((f32[1024,2048]{1,0:T(8,128)}), f32[128,2048]{1,0:T(8,128)}) %reduce-scatter.2.cloned.1.call-update) | async-done | bytes 1048592 | tf_op jit(solution)/shard_map/reduce_scatter | solution.py:90
  253.7 1.3 copy_bitcast_fusion.1
  255.0 0.7 gather_fusion.1
  255.7 1.6 copy_bitcast_fusion
  257.4 7.0 %all-to-all-start = ((f32[16,128,256]{2,1,0:T(8,128)}), f32[16,128,256]{2,1,0:T(8,128)}, u32[]{:S(2)}, u32[]{:S(2)}) async-start(f32[16,128,256]{2,1,0:T(8,128)} %copy_bitcast_fusion), calls=%async_computation.1 | async-start | bytes 4194304 | tf_op jit(solution)/shard_map/all_to_all | solution.py:109
  264.4 0.5 bitcast_reduce_fusion
  264.9 32.2 %psum.7 = f32[16,256]{1,0:T(8,128)S(1)} all-reduce(f32[16,256]{1,0:T(8,128)S(1)} %bitcast.38), channel_id=1, replica_groups=mesh['grp_0'=2,'grp_1'=4,'blk_0'=2,'blk_1'=4,'blk_2'=2] {'grp_0','grp_1'}, use_global_device_ids=true, to_apply=%region_5.6 | all-reduce | flops 4096 | bytes 32768 | tf_op jit(solution)/shard_map/psum | solution.py:110
  297.1 14.8 %all_to_all.14 = f32[16,1,256]{2,1,0:T(1,128)S(1)} all-to-all(f32[16,1,256]{2,1,0:T(1,128)S(1)} %all_to_all.10), channel_id=1, replica_groups=mesh['grp_0'=2,'grp_1'=4,'blk_0'=2,'blk_1'=4,'blk_2'=2] {'blk_0','blk_1'..., dimensions={0} | all-to-all | bytes 32768 | tf_op jit(solution)/shard_map/all_to_all | solution.py:112
  312.0 3.1 divide_bitcast_fusion
  (30 shorter events, 1.0 us)
Async XLA Ops:
  6.5 128.6 %all-gather.2.cloned.1.call-start = ((), (), s32[]{:S(2)}) async-start(), calls=%async_computation.3 | async-start | bytes 17825792 | tf_op jit(solution)/shard_map/all_gather | solution.py:85
  7.9 2.5 copy-start.2
  10.3 243.4 %reduce-scatter.2.cloned.1.call-start = ((), (), s32[]{:S(2)}) async-start(), calls=%async_computation.4 | async-start | bytes 9437184 | tf_op jit(solution)/shard_map/reduce_scatter | solution.py:90
  11.5 2.2 copy-start.1
  135.2 2.2 copy-start
  165.2 0.7 copy-start.3
  257.4 39.8 %all-to-all-start = ((f32[16,128,256]{2,1,0:T(8,128)}), f32[16,128,256]{2,1,0:T(8,128)}, u32[]{:S(2)}, u32[]{:S(2)}) async-start(f32[16,128,256]{2,1,0:T(8,128)} %copy_bitcast_fusion), calls=%async_computation.1 | async-start | bytes 4194304 | tf_op jit(solution)/shard_map/all_to_all | solution.py:109
Sparse Core Ops, SparseCore 0:
  10.5 124.6 all-gather.1
  165.3 88.3 reduce-scatter.1

commit v7 on v4

--- a/solution.py
+++ b/solution.py
@@ -14,7 +14,7 @@
 TILE = 256
 
 
-def expand_kernel(row_blocks, slots_ref, left_ref, right_ref, out_ref):
+def expand_kernel(row_blocks, order, slots_ref, left_ref, right_ref, out_ref):
     step = pl.program_id(0)
     product = jnp.dot(left_ref[...], right_ref[...], preferred_element_type=jnp.float32)
     per_tile = TILE // BS
@@ -24,17 +24,17 @@
 
             @pl.when(slot >= 0)
             def _():
-                out_ref[pl.ds(r * BS, BS), pl.ds(pl.multiple_of(slot * BS, BS), BS)] = product[
+                out_ref[pl.ds(order[r] * BS, BS), pl.ds(pl.multiple_of(slot * BS, BS), BS)] = product[
                     r * BS:(r + 1) * BS, t * BS:(t + 1) * BS
                 ]
 
 
-def expand_packed(slots, left, right, half_blocks):
+def expand_packed(slots, left, right, half_blocks, order):
     rows, inner = left.shape
     width = right.shape[1]
     row_blocks = rows // BS
     return pl.pallas_call(
-        functools.partial(expand_kernel, row_blocks),
+        functools.partial(expand_kernel, row_blocks, order),
         out_shape=jax.ShapeDtypeStruct((rows, half_blocks * BS), jnp.float32),
         grid_spec=pltpu.PrefetchScalarGridSpec(
             num_scalar_prefetch=1,
@@ -86,8 +86,12 @@
     local_pruned = lax.dynamic_slice_in_dim(pruned, blk_id * row_blocks, row_blocks, 0)
     local_slots = jnp.clip(jnp.cumsum(local_pruned, axis=1) - 1, 0, half_blocks - 1)
     slot_table = jnp.where(local_pruned > 0, local_slots, -1).astype(jnp.int32)
-    packed = expand_packed(slot_table, left, gathered, half_blocks)
-    summed_packed = lax.psum_scatter(packed, GRP, scatter_dimension=0, tiled=True)
+    z_size = lax.axis_size(GRP[0])
+    x_size = lax.axis_size(GRP[1])
+    order = tuple((r % x_size) * z_size + r // x_size for r in range(row_blocks))
+    packed = expand_packed(slot_table, left, gathered, half_blocks, order)
+    staged = lax.psum_scatter(packed, GRP[1], scatter_dimension=0, tiled=True)
+    summed_packed = lax.psum_scatter(staged, GRP[0], scatter_dimension=0, tiled=True)
     piece_rows = row_count // lax.axis_size(GRP)
     row_block = (blk_id * row_count + grp_id * piece_rows) // BS
     row_pruned = lax.dynamic_index_in_dim(pruned, row_block, 0, keepdims=False)

time: 320 us -> 345 us (1.078)
  waiting for transfers between devices: 204 us -> 231 us
    reduce_scatter x1 -> x2, waiting for transfers between devices: 85.2 us -> 112 us  [the longest x1 77.2 us: shards(): staged = lax.psum_scatter(packed, GRP[1], scatter_dimension=0, tiled=True)]
  transfers between devices with their start and end apart: 2 -> 3, of which waited for: 2 -> 3; matrix products, arithmetic and copies ran while one was open for 2% -> 2% of each run, Pallas kernels for 0% -> 0%
where the time goes in v7:
time: 345 us; the launch traced here: 343 us
  waiting for transfers between devices  231 us (67%)
  blocking collectives  52.1 us (15%)
  Pallas kernels  27.8 us (8%)
  between operations  13.3 us (4%)
  other arithmetic  10.8 us (3%)
  local copies, waits for them, and re-layouts  8.34 us (2%)
    all_gather x1, waiting for transfers between devices, shards(): gathered = lax.all_gather(right, BLK, axis=1, tiled=True)  119 us
    reduce_scatter x1, waiting for transfers between devices, shards(): staged = lax.psum_scatter(packed, GRP[1], scatter_dimension=0, tiled=True)  77.2 us
    all_to_all x1, blocking collectives, shards(): lax.all_to_all(arranged, BLK, split_axis=0, concat_axis=0, tiled=True)  35.7 us
    reduce_scatter x1, waiting for transfers between devices, shards(): lax.psum_scatter(staged, GRP[0], scatter_dimension=0, tiled=True)  34.9 us
    pallas_call x1, Pallas kernels, expand_packed(): pl.pallas_call(functools.partial(expand_kernel, row_blocks, order), out_s...  27.8 us
    psum x1, blocking collectives, shards(): totals = lax.psum(jnp.sum(moved, axis=(0, 1)), GRP)  16.5 us
  transfers between devices with their start and end apart: 3, of which 3 were waited for; matrix products, arithmetic and copies ran while one was open for 2% of the time, Pallas kernels for 0%

profile of v7, /device:TPU:2, one launch (start us, length us, event | category | flops | bytes accessed | tf_op | source)
XLA Modules:
  0.0 343.2 jit_solution(13909987547736986958)
XLA Ops:
  6.5 0.8 dynamic-slice_convert_fusion
  7.3 0.6 mul.80
  7.9 2.4 bitcast_multiply_fusion.1
  10.5 0.2 reduce_window_sum.18
  10.7 0.8 dynamic-slice_convert_fusion.1
  11.5 0.6 mul.76
  12.1 1.6 copy-done.1
  13.7 2.8 bitcast_multiply_fusion.left_ref
  16.5 118.6 %all-gather.2.cloned.1.call-done.right_ref = bf16[2048,4096]{1,0:T(8,128)(2,1)} async-done(((bf16[2048,256]{1,0:T(8,128)(2,1)}), bf16[2048,4096]{1,0:T(8,128)(2,1)}) %all-gather.2.cloned.1.call-update) | async-done | bytes 16777232 | tf_op jit(solution)/shard_map/all_gather | solution.py:85
  135.2 2.2 copy-done
  137.4 27.8 %shard_map.55 = f32[1024,2048]{1,0:T(8,128)} custom-call(s32[8,32]{1,0:T(8,128)S(1)} %clamp_select_fusion.slots_ref, bf16[1024,2048]{1,0:T(8,128)(2,1)S(1)} %copy-done, bf16[2048,4096]{1,0:T(8,128)(2,1)} %all-gather.2.cloned.1.call-done.right_ref), custom_call_target="tpu_custom_call" | custom-call | flops 17179869184 | bytes 29360128 | tf_op jit(solution)/shard_map/pallas_call | solution.py:36
  165.2 77.2 %reduce-scatter.3.cloned.1.call-done = f32[256,2048]{1,0:T(8,128)} async-done(((f32[1024,2048]{1,0:T(8,128)}), f32[256,2048]{1,0:T(8,128)}) %reduce-scatter.3.cloned.1.call-update) | async-done | bytes 2097168 | tf_op jit(solution)/shard_map/reduce_scatter | solution.py:93
  242.5 0.2 dynamic-slice_reduce_fusion
  242.8 0.7 scatter_custom_fusion
  243.6 0.7 gather_fusion
  244.5 0.7 gather_fusion.2
  245.4 34.9 %reduce-scatter.5.cloned.1.call-done = f32[128,2048]{1,0:T(8,128)} async-done(((f32[256,2048]{1,0:T(8,128)}), f32[128,2048]{1,0:T(8,128)}) %reduce-scatter.5.cloned.1.call-update) | async-done | bytes 1048592 | tf_op jit(solution)/shard_map/reduce_scatter | solution.py:94
  280.3 1.3 copy_bitcast_fusion.1
  281.7 0.7 gather_fusion.1
  282.3 0.3 copy_bitcast_fusion
  282.7 35.7 %all_to_all.5 = f32[16,128,256]{2,1,0:T(8,128)S(1)} all-to-all(f32[16,128,256]{2,1,0:T(8,128)S(1)} %copy_bitcast_fusion), channel_id=1, replica_groups=mesh['grp_0'=2,'grp_1'=4,'blk_0'=2,'blk_1'=4,'blk_2'=2] {'blk_0','blk_1'..., dimensions={0} | all-to-all | bytes 4194304 | tf_op jit(solution)/shard_map/all_to_all | solution.py:113
  318.3 0.3 reduce_sum.9
  318.6 16.5 %psum.7 = f32[256]{0:T(256)S(1)} all-reduce(f32[256]{0:T(256)S(1)} %reduce_sum.9), channel_id=1, replica_groups=mesh['grp_0'=2,'grp_1'=4,'blk_0'=2,'blk_1'=4,'blk_2'=2] {'grp_0','grp_1'}, use_global_device_ids=true, to_apply=%region_6.7 | all-reduce | flops 256 | bytes 2048 | tf_op jit(solution)/shard_map/psum | solution.py:114
  335.1 1.6 divide_bitcast_fusion
  (28 shorter events, 0.9 us)
Async XLA Ops:
  6.5 128.6 %all-gather.2.cloned.1.call-start = ((), (), s32[]{:S(2)}) async-start(), calls=%async_computation.3 | async-start | bytes 17825792 | tf_op jit(solution)/shard_map/all_gather | solution.py:85
  7.9 2.5 copy-start.2
  10.3 232.1 %reduce-scatter.3.cloned.1.call-start = ((), (), s32[]{:S(2)}) async-start(), calls=%async_computation.4 | async-start | bytes 10485760 | tf_op jit(solution)/shard_map/reduce_scatter | solution.py:93
  11.5 2.2 copy-start.1
  135.2 2.2 copy-start
  165.2 77.6 %copy-start.3 = (s32[32]{0:T(128)S(1)}, s32[32]{0:T(128)}, u32[]{:S(2)}) copy-start(s32[32]{0:T(128)} %param.9) | copy-start | bytes 388
  165.2 115.1 %reduce-scatter.5.cloned.1.call-start = ((), (), s32[]{:S(2)}) async-start(), calls=%async_computation.5 | async-start | bytes 3145728 | tf_op jit(solution)/shard_map/reduce_scatter | solution.py:94
Sparse Core Ops, SparseCore 0:
  10.5 124.6 all-gather.1
  165.3 77.1 reduce-scatter.2
  244.8 35.4 reduce-scatter.4

commit v8 on v4

--- a/solution.py
+++ b/solution.py
@@ -11,7 +11,7 @@
 BS = 128
 BLK = ("blk_0", "blk_1", "blk_2")
 GRP = ("grp_0", "grp_1")
-TILE = 256
+TILE = 512
 
 
 def expand_kernel(row_blocks, slots_ref, left_ref, right_ref, out_ref):

time: 320 us -> 319 us (level)
  no operation moved by 1% of the time
where the time goes in v8:
time: 319 us; the launch traced here: 318 us
  waiting for transfers between devices  204 us (64%)
  blocking collectives  54.4 us (17%)
  Pallas kernels  26.9 us (8%)
  between operations  13.5 us (4%)
  other arithmetic  10.8 us (3%)
  local copies, waits for them, and re-layouts  8.7 us (3%)
    all_gather x1, waiting for transfers between devices, shards(): gathered = lax.all_gather(right, BLK, axis=1, tiled=True)  119 us
    reduce_scatter x1, waiting for transfers between devices, shards(): lax.psum_scatter(packed, GRP, scatter_dimension=0, tiled=True)  85.2 us
    all_to_all x1, blocking collectives, shards(): lax.all_to_all(arranged, BLK, split_axis=0, concat_axis=0, tiled=True)  35.9 us
    pallas_call x1, Pallas kernels, expand_packed(): pl.pallas_call(functools.partial(expand_kernel, row_blocks), out_shape=ja...  26.9 us
    psum x1, blocking collectives, shards(): totals = lax.psum(jnp.sum(moved, axis=(0, 1)), GRP)  18.4 us
  transfers between devices with their start and end apart: 2, of which 2 were waited for; matrix products, arithmetic and copies ran while one was open for 2% of the time, Pallas kernels for 0%

profile of v8, /device:TPU:2, one launch (start us, length us, event | category | flops | bytes accessed | tf_op | source)
XLA Modules:
  0.0 318.2 jit_solution(5033387805971584430)
XLA Ops:
  6.5 0.8 dynamic-slice_convert_fusion
  7.3 0.6 mul.80
  7.9 2.4 bitcast_multiply_fusion.1
  10.5 0.2 reduce_window_sum.18
  10.7 0.8 dynamic-slice_convert_fusion.1
  11.5 0.6 mul.76
  12.1 1.6 copy-done.1
  13.7 2.8 bitcast_multiply_fusion.left_ref
  16.5 118.6 %all-gather.2.cloned.1.call-done.right_ref = bf16[2048,4096]{1,0:T(8,128)(2,1)} async-done(((bf16[2048,256]{1,0:T(8,128)(2,1)}), bf16[2048,4096]{1,0:T(8,128)(2,1)}) %all-gather.2.cloned.1.call-update) | async-done | bytes 16777232 | tf_op jit(solution)/shard_map/all_gather | solution.py:85
  135.2 2.2 copy-done
  137.4 26.9 %shard_map.55 = f32[1024,2048]{1,0:T(8,128)} custom-call(s32[8,32]{1,0:T(8,128)S(1)} %clamp_select_fusion.slots_ref, bf16[1024,2048]{1,0:T(8,128)(2,1)S(1)} %copy-done, bf16[2048,4096]{1,0:T(8,128)(2,1)} %all-gather.2.cloned.1.call-done.right_ref), custom_call_target="tpu_custom_call" | custom-call | flops 17179869184 | bytes 29360128 | tf_op jit(solution)/shard_map/pallas_call | solution.py:36
  164.3 0.2 dynamic-slice_reduce_fusion
  164.6 0.4 copy-done.3
  164.9 0.7 scatter_custom_fusion
  165.8 0.7 gather_fusion
  166.6 0.7 gather_fusion.2
  167.6 85.2 %reduce-scatter.2.cloned.1.call-done = f32[128,2048]{1,0:T(8,128)} async-done(((f32[1024,2048]{1,0:T(8,128)}), f32[128,2048]{1,0:T(8,128)}) %reduce-scatter.2.cloned.1.call-update) | async-done | bytes 1048592 | tf_op jit(solution)/shard_map/reduce_scatter | solution.py:90
  252.8 1.3 copy_bitcast_fusion.1
  254.2 0.7 gather_fusion.1
  254.9 0.3 copy_bitcast_fusion
  255.2 35.9 %all_to_all.5 = f32[16,128,256]{2,1,0:T(8,128)S(1)} all-to-all(f32[16,128,256]{2,1,0:T(8,128)S(1)} %copy_bitcast_fusion), channel_id=1, replica_groups=mesh['grp_0'=2,'grp_1'=4,'blk_0'=2,'blk_1'=4,'blk_2'=2] {'blk_0','blk_1'..., dimensions={0} | all-to-all | bytes 4194304 | tf_op jit(solution)/shard_map/all_to_all | solution.py:109
  291.1 0.3 reduce_sum.9
  291.4 18.4 %psum.7 = f32[256]{0:T(256)S(1)} all-reduce(f32[256]{0:T(256)S(1)} %reduce_sum.9), channel_id=1, replica_groups=mesh['grp_0'=2,'grp_1'=4,'blk_0'=2,'blk_1'=4,'blk_2'=2] {'grp_0','grp_1'}, use_global_device_ids=true, to_apply=%region_5.6 | all-reduce | flops 256 | bytes 2048 | tf_op jit(solution)/shard_map/psum | solution.py:110
  309.8 1.6 divide_bitcast_fusion
  (25 shorter events, 0.8 us)
Async XLA Ops:
  6.5 128.6 %all-gather.2.cloned.1.call-start = ((), (), s32[]{:S(2)}) async-start(), calls=%async_computation.2 | async-start | bytes 17825792 | tf_op jit(solution)/shard_map/all_gather | solution.py:85
  7.9 2.5 copy-start.2
  10.3 242.5 %reduce-scatter.2.cloned.1.call-start = ((), (), s32[]{:S(2)}) async-start(), calls=%async_computation.3 | async-start | bytes 9437184 | tf_op jit(solution)/shard_map/reduce_scatter | solution.py:90
  11.5 2.2 copy-start.1
  135.2 2.2 copy-start
  164.3 0.7 copy-start.3
Sparse Core Ops, SparseCore 0:
  10.5 124.6 all-gather.1
  164.4 88.3 reduce-scatter.1

commit v9 on v8

--- a/solution.py
+++ b/solution.py
@@ -107,7 +107,7 @@
         .reshape(blk_count, piece_rows, panel_width)
     )
     moved = lax.all_to_all(arranged, BLK, split_axis=0, concat_axis=0, tiled=True)
-    totals = lax.psum(jnp.sum(moved, axis=(0, 1)), GRP)
+    totals = jnp.sum(lax.all_gather(jnp.sum(moved, axis=(0, 1)), GRP), axis=0)
     normalized = (row_count * blk_count) * moved / totals
     return normalized[:, None, :, :]
 

time: 319 us -> 318 us (level)
    psum x1 -> x0, blocking collectives: 18.4 us -> none  [shards(): totals = lax.psum(jnp.sum(moved, axis=(0, 1)), GRP)]
    all_gather x0 -> x1, blocking collectives: none -> 17.6 us  [shards(): totals = jnp.sum(lax.all_gather(jnp.sum(moved, axis=(0, 1)), GRP), axis=0)]
where the time goes in v9:
time: 318 us; the launch traced here: 317 us
  waiting for transfers between devices  204 us (64%)
  blocking collectives  53.5 us (17%)
  Pallas kernels  26.9 us (8%)
  between operations  13.5 us (4%)
  other arithmetic  10.8 us (3%)
  local copies, waits for them, and re-layouts  8.7 us (3%)
    all_gather x1, waiting for transfers between devices, shards(): gathered = lax.all_gather(right, BLK, axis=1, tiled=True)  119 us
    reduce_scatter x1, waiting for transfers between devices, shards(): lax.psum_scatter(packed, GRP, scatter_dimension=0, tiled=True)  85.2 us
    all_to_all x1, blocking collectives, shards(): lax.all_to_all(arranged, BLK, split_axis=0, concat_axis=0, tiled=True)  36 us
    pallas_call x1, Pallas kernels, expand_packed(): pl.pallas_call(functools.partial(expand_kernel, row_blocks), out_shape=ja...  26.9 us
    all_gather x1, blocking collectives, shards(): totals = jnp.sum(lax.all_gather(jnp.sum(moved, axis=(0, 1)), GRP), axis=0)  17.6 us
  transfers between devices with their start and end apart: 2, of which 2 were waited for; matrix products, arithmetic and copies ran while one was open for 2% of the time, Pallas kernels for 0%

profile of v9, /device:TPU:2, one launch (start us, length us, event | category | flops | bytes accessed | tf_op | source)
XLA Modules:
  0.0 317.5 jit_solution(11281927037684638568)
XLA Ops:
  6.5 0.8 dynamic-slice_convert_fusion
  7.3 0.6 mul.80
  7.9 2.4 bitcast_multiply_fusion.1
  10.5 0.2 reduce_window_sum.18
  10.7 0.8 dynamic-slice_convert_fusion.1
  11.5 0.6 mul.76
  12.1 1.6 copy-done.1
  13.7 2.8 bitcast_multiply_fusion.left_ref
  16.5 118.6 %all-gather.4.cloned.1.call-done.right_ref = bf16[2048,4096]{1,0:T(8,128)(2,1)} async-done(((bf16[2048,256]{1,0:T(8,128)(2,1)}), bf16[2048,4096]{1,0:T(8,128)(2,1)}) %all-gather.4.cloned.1.call-update) | async-done | bytes 16777232 | tf_op jit(solution)/shard_map/all_gather | solution.py:85
  135.2 2.2 copy-done
  137.4 26.9 %shard_map.55 = f32[1024,2048]{1,0:T(8,128)} custom-call(s32[8,32]{1,0:T(8,128)S(1)} %clamp_select_fusion.slots_ref, bf16[1024,2048]{1,0:T(8,128)(2,1)S(1)} %copy-done, bf16[2048,4096]{1,0:T(8,128)(2,1)} %all-gather.4.cloned.1.call-done.right_ref), custom_call_target="tpu_custom_call" | custom-call | flops 17179869184 | bytes 29360128 | tf_op jit(solution)/shard_map/pallas_call | solution.py:36
  164.3 0.2 dynamic-slice_reduce_fusion
  164.6 0.4 copy-done.3
  164.9 0.7 scatter_custom_fusion
  165.7 0.7 gather_fusion
  166.6 0.7 gather_fusion.2
  167.6 85.2 %reduce-scatter.2.cloned.1.call-done = f32[128,2048]{1,0:T(8,128)} async-done(((f32[1024,2048]{1,0:T(8,128)}), f32[128,2048]{1,0:T(8,128)}) %reduce-scatter.2.cloned.1.call-update) | async-done | bytes 1048592 | tf_op jit(solution)/shard_map/reduce_scatter | solution.py:90
  252.8 1.3 copy_bitcast_fusion.1
  254.2 0.7 gather_fusion.1
  254.8 0.3 copy_bitcast_fusion
  255.2 36.0 %all_to_all.5 = f32[16,128,256]{2,1,0:T(8,128)S(1)} all-to-all(f32[16,128,256]{2,1,0:T(8,128)S(1)} %copy_bitcast_fusion), channel_id=1, replica_groups=mesh['grp_0'=2,'grp_1'=4,'blk_0'=2,'blk_1'=4,'blk_2'=2] {'blk_0','blk_1'..., dimensions={0} | all-to-all | bytes 4194304 | tf_op jit(solution)/shard_map/all_to_all | solution.py:109
  291.1 0.3 reduce_sum.18
  291.4 17.6 %all-gather.1 = f32[8,1,256]{2,1,0:T(1,128)S(1)} all-gather(f32[1,1,256]{2,1,0:T(1,128)S(1)} %bitcast.32), channel_id=2, replica_groups=mesh['grp_0'=2,'grp_1'=4,'blk_0'=2,'blk_1'=4,'blk_2'=2] {'grp_0','grp_1'}, dimensions={0}, use_global_device_ids=true | all-gather | bytes 9216 | tf_op jit(solution)/shard_map/all_gather | solution.py:110
  309.0 1.6 divide_bitcast_fusion
  (26 shorter events, 0.8 us)
Async XLA Ops:
  6.5 128.6 %all-gather.4.cloned.1.call-start = ((), (), s32[]{:S(2)}) async-start(), calls=%async_computation.2 | async-start | bytes 17825792 | tf_op jit(solution)/shard_map/all_gather | solution.py:85
  7.9 2.5 copy-start.2
  10.3 242.5 %reduce-scatter.2.cloned.1.call-start = ((), (), s32[]{:S(2)}) async-start(), calls=%async_computation.3 | async-start | bytes 9437184 | tf_op jit(solution)/shard_map/reduce_scatter | solution.py:90
  11.5 2.2 copy-start.1
  135.2 2.2 copy-start
  164.3 0.7 copy-start.3
Sparse Core Ops, SparseCore 0:
  10.5 124.6 all-gather.3
  164.4 88.3 reduce-scatter.1

commit v10 on v9

--- a/solution.py
+++ b/solution.py
@@ -107,7 +107,8 @@
         .reshape(blk_count, piece_rows, panel_width)
     )
     moved = lax.all_to_all(arranged, BLK, split_axis=0, concat_axis=0, tiled=True)
-    totals = jnp.sum(lax.all_gather(jnp.sum(moved, axis=(0, 1)), GRP), axis=0)
+    group_sums = lax.psum(jnp.sum(arranged, axis=1), GRP)
+    totals = lax.psum_scatter(group_sums, BLK, scatter_dimension=0, tiled=True)
     normalized = (row_count * blk_count) * moved / totals
     return normalized[:, None, :, :]
 

time: 318 us -> 380 us (1.19)
  blocking collectives: 53.5 us -> 104 us
  starting transfers between devices: 0.04 us -> 7.19 us
    unnamed x0 -> x1, blocking collectives: none -> 85.6 us
    all_to_all x1 -> x0, blocking collectives: 36 us -> none  [shards(): lax.all_to_all(arranged, BLK, split_axis=0, concat_axis=0, tiled=True)]
    psum x0 -> x1, blocking collectives: none -> 18.4 us  [shards(): group_sums = lax.psum(jnp.sum(arranged, axis=1), GRP)]
    all_gather x1 -> x0, blocking collectives: 17.6 us -> none  [shards(): totals = jnp.sum(lax.all_gather(jnp.sum(moved, axis=(0, 1)), GRP), axis=0)]
    all_to_all x0 -> x1, starting transfers between devices: none -> 7.14 us  [shards(): lax.all_to_all(arranged, BLK, split_axis=0, concat_axis=0, tiled=True)]
  transfers between devices with their start and end apart: 2 -> 3, of which waited for: 2 -> 2; matrix products, arithmetic and copies ran while one was open for 2% -> 2% of each run, Pallas kernels for 0% -> 0%
where the time goes in v10:
time: 380 us; the launch traced here: 379 us
  waiting for transfers between devices  204 us (54%)
  blocking collectives  104 us (27%)
  Pallas kernels  26.9 us (7%)
  other arithmetic  13.8 us (4%)
  between operations  13.6 us (4%)
  local copies, waits for them, and re-layouts  9.92 us (3%)
  starting transfers between devices  7.19 us (2%)
    all_gather x1, waiting for transfers between devices, shards(): gathered = lax.all_gather(right, BLK, axis=1, tiled=True)  119 us
    unnamed x1, blocking collectives  85.6 us
    reduce_scatter x1, waiting for transfers between devices, shards(): lax.psum_scatter(packed, GRP, scatter_dimension=0, tiled=True)  85.2 us
    pallas_call x1, Pallas kernels, expand_packed(): pl.pallas_call(functools.partial(expand_kernel, row_blocks), out_shape=ja...  26.9 us
    psum x1, blocking collectives, shards(): group_sums = lax.psum(jnp.sum(arranged, axis=1), GRP)  18.4 us
  transfers between devices with their start and end apart: 3, of which 2 were waited for; matrix products, arithmetic and copies ran while one was open for 2% of the time, Pallas kernels for 0%

profile of v10, /device:TPU:2, one launch (start us, length us, event | category | flops | bytes accessed | tf_op | source)
XLA Modules:
  0.0 379.3 jit_solution(479849097035025377)
XLA Ops:
  6.5 0.8 dynamic-slice_convert_fusion
  7.3 0.6 mul.80
  7.9 2.4 bitcast_multiply_fusion.1
  10.7 0.8 dynamic-slice_convert_fusion.1
  11.5 0.6 mul.76
  12.1 1.6 copy-done.1
  13.7 2.8 bitcast_multiply_fusion.left_ref
  16.5 118.6 %all-gather.2.cloned.1.call-done.right_ref = bf16[2048,4096]{1,0:T(8,128)(2,1)} async-done(((bf16[2048,256]{1,0:T(8,128)(2,1)}), bf16[2048,4096]{1,0:T(8,128)(2,1)}) %all-gather.2.cloned.1.call-update) | async-done | bytes 16777232 | tf_op jit(solution)/shard_map/all_gather | solution.py:85
  135.2 2.2 copy-done
  137.4 26.9 %shard_map.55 = f32[1024,2048]{1,0:T(8,128)} custom-call(s32[8,32]{1,0:T(8,128)S(1)} %clamp_select_fusion.slots_ref, bf16[1024,2048]{1,0:T(8,128)(2,1)S(1)} %copy-done, bf16[2048,4096]{1,0:T(8,128)(2,1)} %all-gather.2.cloned.1.call-done.right_ref), custom_call_target="tpu_custom_call" | custom-call | flops 17179869184 | bytes 29360128 | tf_op jit(solution)/shard_map/pallas_call | solution.py:36
  164.9 0.7 scatter_custom_fusion
  165.8 0.7 gather_fusion
  166.6 0.7 gather_fusion.2
  167.6 85.2 %reduce-scatter.2.cloned.1.call-done = f32[128,2048]{1,0:T(8,128)} async-done(((f32[1024,2048]{1,0:T(8,128)}), f32[128,2048]{1,0:T(8,128)}) %reduce-scatter.2.cloned.1.call-update) | async-done | bytes 1048592 | tf_op jit(solution)/shard_map/reduce_scatter | solution.py:90
  252.8 1.3 copy_bitcast_fusion.1
  254.2 0.7 gather_fusion.1
  254.9 1.6 copy_bitcast_fusion
  256.5 7.1 %all-to-all-start = ((f32[16,128,256]{2,1,0:T(8,128)}), f32[16,128,256]{2,1,0:T(8,128)}, u32[]{:S(2)}, u32[]{:S(2)}) async-start(f32[16,128,256]{2,1,0:T(8,128)} %copy_bitcast_fusion), calls=%async_computation.1 | async-start | bytes 4194304 | tf_op jit(solution)/shard_map/all_to_all | solution.py:109
  263.6 0.6 dynamic-slice
  264.2 0.5 bitcast_reduce_fusion
  264.7 85.6 %all-reduce = f32[16,256]{1,0:T(8,128)S(1)} all-reduce(f32[16,256]{1,0:T(8,128)S(1)} %bitcast.40), channel_id=3, replica_groups=mesh['grp_0'=2,'grp_1'=4,'blk_0'=2,'blk_1'=4,'blk_2'=2] {'blk_0','blk_1'..., use_global_device_ids=true, to_apply=%region_6.7.clone | all-reduce | flops 4096 | bytes 32768
  350.3 0.6 constant_dynamic-slice_fusion
  351.0 18.4 %psum.8 = f32[1,256]{1,0:T(1,128)S(1)} all-reduce(f32[1,256]{1,0:T(1,128)S(1)} %constant_dynamic-slice_fusion), channel_id=1, replica_groups=mesh['grp_0'=2,'grp_1'=4,'blk_0'=2,'blk_1'=4,'blk_2'=2] {'grp_0','grp_1'}, use_global_device_ids=true, to_apply=%region_5.6 | all-reduce | flops 256 | bytes 2048 | tf_op jit(solution)/shard_map/psum | solution.py:110
  369.4 3.1 divide_bitcast_fusion
  (32 shorter events, 1.6 us)
Async XLA Ops:
  6.5 128.6 %all-gather.2.cloned.1.call-start = ((), (), s32[]{:S(2)}) async-start(), calls=%async_computation.2 | async-start | bytes 17825792 | tf_op jit(solution)/shard_map/all_gather | solution.py:85
  7.9 2.5 copy-start.2
  10.3 242.5 %reduce-scatter.2.cloned.1.call-start = ((), (), s32[]{:S(2)}) async-start(), calls=%async_computation.3 | async-start | bytes 9437184 | tf_op jit(solution)/shard_map/reduce_scatter | solution.py:90
  11.5 2.2 copy-start.1
  135.2 2.2 copy-start
  164.3 0.7 copy-start.3
  256.5 7.2 %copy-start.4 = (u32[128]{0:T(128)S(1)}, u32[128]{0:T(128)}, u32[]{:S(2)}) copy-start(u32[128]{0:T(128)} %constant.87) | copy-start | bytes 1540
  256.5 112.9 %all-to-all-start = ((f32[16,128,256]{2,1,0:T(8,128)}), f32[16,128,256]{2,1,0:T(8,128)}, u32[]{:S(2)}, u32[]{:S(2)}) async-start(f32[16,128,256]{2,1,0:T(8,128)} %copy_bitcast_fusion), calls=%async_computation.1 | async-start | bytes 4194304 | tf_op jit(solution)/shard_map/all_to_all | solution.py:109
Sparse Core Ops, SparseCore 0:
  10.5 124.6 all-gather.1
  164.4 88.3 reduce-scatter.1

commit v11 on v9

--- a/solution.py
+++ b/solution.py
@@ -78,10 +78,9 @@
     )
     tile_right = lax.dynamic_slice(
         pattern, (grp_id * inner_blocks, blk_id * panel_blocks), (inner_blocks, panel_blocks)
-    ).astype(jnp.bfloat16)
-    right = (
-        panels.reshape(inner_blocks, BS, panel_blocks, BS) * tile_right[:, None, :, None]
-    ).reshape(inner, panel_width)
+    )
+    keep_right = jnp.repeat(jnp.repeat(tile_right > 0, BS, axis=0), BS, axis=1)
+    right = jnp.where(keep_right, panels, jnp.zeros_like(panels))
     gathered = lax.all_gather(right, BLK, axis=1, tiled=True)
     local_pruned = lax.dynamic_slice_in_dim(pruned, blk_id * row_blocks, row_blocks, 0)
     local_slots = jnp.clip(jnp.cumsum(local_pruned, axis=1) - 1, 0, half_blocks - 1)

time: 318 us -> 317 us (level)
  no operation moved by 1% of the time
where the time goes in v11:
time: 317 us
  waiting for transfers between devices  204 us (64%)
  blocking collectives  53.5 us (17%)
  Pallas kernels  26.9 us (8%)
  between operations  13.6 us (4%)
  other arithmetic  9.58 us (3%)
  local copies, waits for them, and re-layouts  9.45 us (3%)
    all_gather x1, waiting for transfers between devices, shards(): gathered = lax.all_gather(right, BLK, axis=1, tiled=True)  119 us
    reduce_scatter x1, waiting for transfers between devices, shards(): lax.psum_scatter(packed, GRP, scatter_dimension=0, tiled=True)  85.2 us
    all_to_all x1, blocking collectives, shards(): lax.all_to_all(arranged, BLK, split_axis=0, concat_axis=0, tiled=True)  36 us
    pallas_call x1, Pallas kernels, expand_packed(): pl.pallas_call(functools.partial(expand_kernel, row_blocks), out_shape=ja...  26.9 us
    all_gather x1, blocking collectives, shards(): totals = jnp.sum(lax.all_gather(jnp.sum(moved, axis=(0, 1)), GRP), axis=0)  17.6 us
  transfers between devices with their start and end apart: 2, of which 2 were waited for; matrix products, arithmetic and copies ran while one was open for 2% of the time, Pallas kernels for 0%

profile of v11, /device:TPU:2, one launch (start us, length us, event | category | flops | bytes accessed | tf_op | source)
XLA Modules:
  0.0 317.0 jit_solution(11322957977916121740)
XLA Ops:
  6.5 0.9 dynamic-slice_compare_fusion
  7.6 0.2 broadcast_in_dim.38
  7.8 1.0 copy.24
  8.8 1.1 broadcast_select_fusion
  10.1 0.2 reduce_window_sum.18
  10.3 0.8 dynamic-slice_convert_fusion
  11.1 0.6 mul.65
  11.7 1.6 copy-done.1
  13.3 2.8 bitcast_multiply_fusion.left_ref
  16.1 118.6 %all-gather.4.cloned.1.call-done.right_ref = bf16[2048,4096]{1,0:T(8,128)(2,1)} async-done(((bf16[2048,256]{1,0:T(8,128)(2,1)}), bf16[2048,4096]{1,0:T(8,128)(2,1)}) %all-gather.4.cloned.1.call-update) | async-done | bytes 16777232 | tf_op jit(solution)/shard_map/all_gather | solution.py:84
  134.7 2.2 copy-done
  136.9 26.9 %shard_map.55 = f32[1024,2048]{1,0:T(8,128)} custom-call(s32[8,32]{1,0:T(8,128)S(1)} %clamp_select_fusion.slots_ref, bf16[1024,2048]{1,0:T(8,128)(2,1)S(1)} %copy-done, bf16[2048,4096]{1,0:T(8,128)(2,1)} %all-gather.4.cloned.1.call-done.right_ref), custom_call_target="tpu_custom_call" | custom-call | flops 17179869184 | bytes 29360128 | tf_op jit(solution)/shard_map/pallas_call | solution.py:36
  164.1 0.4 copy-done.4
  164.5 0.7 scatter_custom_fusion
  165.3 0.7 gather_fusion
  166.2 0.7 gather_fusion.2
  167.1 85.2 %reduce-scatter.2.cloned.1.call-done = f32[128,2048]{1,0:T(8,128)} async-done(((f32[1024,2048]{1,0:T(8,128)}), f32[128,2048]{1,0:T(8,128)}) %reduce-scatter.2.cloned.1.call-update) | async-done | bytes 1048592 | tf_op jit(solution)/shard_map/reduce_scatter | solution.py:89
  252.4 1.3 copy_bitcast_fusion.1
  253.7 0.7 gather_fusion.1
  254.4 0.3 copy_bitcast_fusion
  254.7 36.0 %all_to_all.5 = f32[16,128,256]{2,1,0:T(8,128)S(1)} all-to-all(f32[16,128,256]{2,1,0:T(8,128)S(1)} %copy_bitcast_fusion), channel_id=1, replica_groups=mesh['grp_0'=2,'grp_1'=4,'blk_0'=2,'blk_1'=4,'blk_2'=2] {'blk_0','blk_1'..., dimensions={0} | all-to-all | bytes 4194304 | tf_op jit(solution)/shard_map/all_to_all | solution.py:108
  290.7 0.3 reduce_sum.18
  291.0 17.6 %all-gather.1 = f32[8,1,256]{2,1,0:T(1,128)S(1)} all-gather(f32[1,1,256]{2,1,0:T(1,128)S(1)} %bitcast.37), channel_id=2, replica_groups=mesh['grp_0'=2,'grp_1'=4,'blk_0'=2,'blk_1'=4,'blk_2'=2] {'grp_0','grp_1'}, dimensions={0}, use_global_device_ids=true | all-gather | bytes 9216 | tf_op jit(solution)/shard_map/all_gather | solution.py:109
  308.6 1.6 divide_bitcast_fusion
  (32 shorter events, 1.2 us)
Async XLA Ops:
  6.5 2.2 copy-start.2
  6.5 128.2 %all-gather.4.cloned.1.call-start = ((), (), s32[]{:S(2)}) async-start(), calls=%async_computation.2 | async-start | bytes 17825792 | tf_op jit(solution)/shard_map/all_gather | solution.py:84
  8.8 1.2 copy-start.3
  9.9 242.5 %reduce-scatter.2.cloned.1.call-start = ((), (), s32[]{:S(2)}) async-start(), calls=%async_computation.3 | async-start | bytes 9437184 | tf_op jit(solution)/shard_map/reduce_scatter | solution.py:89
  11.1 2.2 copy-start.1
  134.7 2.2 copy-start
  163.8 0.7 copy-start.4
Sparse Core Ops, SparseCore 0:
  10.0 124.6 all-gather.3
  164.0 88.3 reduce-scatter.1

commit v12 on v9

--- a/solution.py
+++ b/solution.py
@@ -106,7 +106,13 @@
         .transpose(1, 0, 2, 3)
         .reshape(blk_count, piece_rows, panel_width)
     )
-    moved = lax.all_to_all(arranged, BLK, split_axis=0, concat_axis=0, tiled=True)
+    cores = lax.axis_size(BLK[2])
+    chips = blk_count // cores
+    moved = lax.all_to_all(
+        arranged.reshape(chips, cores, piece_rows, panel_width), BLK[:2], 0, 0, tiled=True
+    )
+    moved = lax.all_to_all(moved.transpose(1, 0, 2, 3), BLK[2], 0, 0, tiled=True)
+    moved = moved.transpose(1, 0, 2, 3).reshape(blk_count, piece_rows, panel_width)
     totals = jnp.sum(lax.all_gather(jnp.sum(moved, axis=(0, 1)), GRP), axis=0)
     normalized = (row_count * blk_count) * moved / totals
     return normalized[:, None, :, :]

time: 318 us -> 332 us (1.044)
  local copies, waits for them, and re-layouts: 8.7 us -> 13.9 us
  blocking collectives: 53.5 us -> 58.1 us
  other arithmetic: 10.8 us -> 15.3 us
    all_to_all x1 -> x2, blocking collectives: 36 us -> 40.5 us  [the longest x1 35.1 us: shards(): lax.all_to_all(arranged.reshape(chips, cores, piece_rows, panel_width), B...]
    mul x0 -> x2, other arithmetic: none -> 3.35 us  [the longest x1 3.08 us: shards(): normalized = row_count * blk_count * moved / totals]
where the time goes in v12:
time: 332 us
  waiting for transfers between devices  204 us (61%)
  blocking collectives  58.1 us (18%)
  Pallas kernels  26.9 us (8%)
  other arithmetic  15.3 us (5%)
  local copies, waits for them, and re-layouts  13.9 us (4%)
  between operations  13.5 us (4%)
    all_gather x1, waiting for transfers between devices, shards(): gathered = lax.all_gather(right, BLK, axis=1, tiled=True)  119 us
    reduce_scatter x1, waiting for transfers between devices, shards(): lax.psum_scatter(packed, GRP, scatter_dimension=0, tiled=True)  85.2 us
    all_to_all x1, blocking collectives, shards(): lax.all_to_all(arranged.reshape(chips, cores, piece_rows, panel_width), B...  35.1 us
    pallas_call x1, Pallas kernels, expand_packed(): pl.pallas_call(functools.partial(expand_kernel, row_blocks), out_shape=ja...  26.9 us
    all_gather x1, blocking collectives, shards(): totals = jnp.sum(lax.all_gather(jnp.sum(moved, axis=(0, 1)), GRP), axis=0)  17.6 us
  transfers between devices with their start and end apart: 2, of which 2 were waited for; matrix products, arithmetic and copies ran while one was open for 2% of the time, Pallas kernels for 0%

profile of v12, /device:TPU:2, one launch (start us, length us, event | category | flops | bytes accessed | tf_op | source)
XLA Modules:
  0.0 331.7 jit_solution(12343347364440635032)
XLA Ops:
  6.5 0.8 dynamic-slice_convert_fusion
  7.3 0.6 mul.93
  7.9 2.4 bitcast_multiply_fusion.1
  10.7 0.8 dynamic-slice_convert_fusion.1
  11.5 0.6 mul.89
  12.1 1.6 copy-done.1
  13.7 2.8 bitcast_multiply_fusion.left_ref
  16.5 118.6 %all-gather.4.cloned.1.call-done.right_ref = bf16[2048,4096]{1,0:T(8,128)(2,1)} async-done(((bf16[2048,256]{1,0:T(8,128)(2,1)}), bf16[2048,4096]{1,0:T(8,128)(2,1)}) %all-gather.4.cloned.1.call-update) | async-done | bytes 16777232 | tf_op jit(solution)/shard_map/all_gather | solution.py:85
  135.2 2.2 copy-done
  137.4 26.9 %shard_map.55 = f32[1024,2048]{1,0:T(8,128)} custom-call(s32[8,32]{1,0:T(8,128)S(1)} %clamp_select_fusion.slots_ref, bf16[1024,2048]{1,0:T(8,128)(2,1)S(1)} %copy-done, bf16[2048,4096]{1,0:T(8,128)(2,1)} %all-gather.4.cloned.1.call-done.right_ref), custom_call_target="tpu_custom_call" | custom-call | flops 17179869184 | bytes 29360128 | tf_op jit(solution)/shard_map/pallas_call | solution.py:36
  164.6 0.4 copy-done.3
  164.9 0.7 scatter_custom_fusion
  165.7 0.7 gather_fusion
  166.6 0.7 gather_fusion.2
  167.6 85.2 %reduce-scatter.2.cloned.1.call-done = f32[128,2048]{1,0:T(8,128)} async-done(((f32[1024,2048]{1,0:T(8,128)}), f32[128,2048]{1,0:T(8,128)}) %reduce-scatter.2.cloned.1.call-update) | async-done | bytes 1048592 | tf_op jit(solution)/shard_map/reduce_scatter | solution.py:90
  252.8 1.3 copy_bitcast_fusion
  254.2 2.0 gather_fusion.1
  256.2 1.9 copy.40
  258.4 35.1 %all_to_all.10 = f32[8,2,128,256]{2,3,1,0:T(8,128)S(1)} all-to-all(f32[8,2,128,256]{2,3,1,0:T(8,128)S(1)} %bitcast.35), channel_id=1, replica_groups=mesh['grp_0'=2,'grp_1'=4,'blk_0'=2,'blk_1'=4,'blk_2'=2] {'blk_0','blk_1'}, dimensions={0} | all-to-all | bytes 4194304 | tf_op jit(solution)/shard_map/all_to_all | solution.py:111
  293.6 5.4 %all_to_all.11 = f32[2,8,128,256]{2,3,1,0:T(8,128)S(1)} all-to-all(f32[2,8,128,256]{2,3,1,0:T(8,128)S(1)} %copy.41), channel_id=1, replica_groups=mesh['grp_0'=2,'grp_1'=4,'blk_0'=2,'blk_1'=4,'blk_2'=2] {'blk_2'}, dimensions={0} | all-to-all | bytes 4194304 | tf_op jit(solution)/shard_map/all_to_all | solution.py:114
  299.0 1.8 copy.42
  300.8 3.1 broadcast_multiply_fusion
  304.1 17.6 %all-gather.1 = f32[8,1,256]{2,1,0:T(1,128)S(1)} all-gather(f32[1,1,256]{2,1,0:T(1,128)S(1)} %bitcast.40), channel_id=2, replica_groups=mesh['grp_0'=2,'grp_1'=4,'blk_0'=2,'blk_1'=4,'blk_2'=2] {'grp_0','grp_1'}, dimensions={0}, use_global_device_ids=true | all-gather | bytes 9216 | tf_op jit(solution)/shard_map/all_gather | solution.py:116
  321.7 3.1 fusion
  (31 shorter events, 1.9 us)
Async XLA Ops:
  6.5 128.6 %all-gather.4.cloned.1.call-start = ((), (), s32[]{:S(2)}) async-start(), calls=%async_computation.3 | async-start | bytes 17825792 | tf_op jit(solution)/shard_map/all_gather | solution.py:85
  7.9 2.5 copy-start.2
  10.3 242.5 %reduce-scatter.2.cloned.1.call-start = ((), (), s32[]{:S(2)}) async-start(), calls=%async_computation.4 | async-start | bytes 9437184 | tf_op jit(solution)/shard_map/reduce_scatter | solution.py:90
  11.5 2.2 copy-start.1
  135.2 2.2 copy-start
  164.3 0.7 copy-start.3
Sparse Core Ops, SparseCore 0:
  10.5 124.6 all-gather.3
  164.4 88.3 reduce-scatter.1

commit v13 on v9

--- a/solution.py
+++ b/solution.py
@@ -11,7 +11,7 @@
 BS = 128
 BLK = ("blk_0", "blk_1", "blk_2")
 GRP = ("grp_0", "grp_1")
-TILE = 512
+TILE = 1024
 
 
 def expand_kernel(row_blocks, slots_ref, left_ref, right_ref, out_ref):

time: 318 us -> 318 us (level)
  no operation moved by 1% of the time
where the time goes in v13:
time: 318 us; the launch traced here: 317 us
  waiting for transfers between devices  204 us (64%)
  blocking collectives  53.6 us (17%)
  Pallas kernels  26.8 us (8%)
  between operations  13.5 us (4%)
  other arithmetic  10.8 us (3%)
  local copies, waits for them, and re-layouts  8.7 us (3%)
    all_gather x1, waiting for transfers between devices, shards(): gathered = lax.all_gather(right, BLK, axis=1, tiled=True)  119 us
    reduce_scatter x1, waiting for transfers between devices, shards(): lax.psum_scatter(packed, GRP, scatter_dimension=0, tiled=True)  85.2 us
    all_to_all x1, blocking collectives, shards(): lax.all_to_all(arranged, BLK, split_axis=0, concat_axis=0, tiled=True)  36 us
    pallas_call x1, Pallas kernels, expand_packed(): pl.pallas_call(functools.partial(expand_kernel, row_blocks), out_shape=ja...  26.8 us
    all_gather x1, blocking collectives, shards(): totals = jnp.sum(lax.all_gather(jnp.sum(moved, axis=(0, 1)), GRP), axis=0)  17.6 us
  transfers between devices with their start and end apart: 2, of which 2 were waited for; matrix products, arithmetic and copies ran while one was open for 2% of the time, Pallas kernels for 0%

profile of v13, /device:TPU:2, one launch (start us, length us, event | category | flops | bytes accessed | tf_op | source)
XLA Modules:
  0.0 317.4 jit_solution(9074511839806146817)
XLA Ops:
  6.5 0.8 dynamic-slice_convert_fusion
  7.3 0.6 mul.80
  7.9 2.4 bitcast_multiply_fusion.1
  10.5 0.2 reduce_window_sum.18
  10.7 0.8 dynamic-slice_convert_fusion.1
  11.5 0.6 mul.76
  12.1 1.6 copy-done.1
  13.7 2.8 bitcast_multiply_fusion.left_ref
  16.5 118.6 %all-gather.4.cloned.1.call-done.right_ref = bf16[2048,4096]{1,0:T(8,128)(2,1)} async-done(((bf16[2048,256]{1,0:T(8,128)(2,1)}), bf16[2048,4096]{1,0:T(8,128)(2,1)}) %all-gather.4.cloned.1.call-update) | async-done | bytes 16777232 | tf_op jit(solution)/shard_map/all_gather | solution.py:85
  135.2 2.2 copy-done
  137.4 26.8 %shard_map.55 = f32[1024,2048]{1,0:T(8,128)} custom-call(s32[8,32]{1,0:T(8,128)S(1)} %clamp_select_fusion.slots_ref, bf16[1024,2048]{1,0:T(8,128)(2,1)S(1)} %copy-done, bf16[2048,4096]{1,0:T(8,128)(2,1)} %all-gather.4.cloned.1.call-done.right_ref), custom_call_target="tpu_custom_call" | custom-call | flops 17179869184 | bytes 29360128 | tf_op jit(solution)/shard_map/pallas_call | solution.py:36
  164.2 0.2 dynamic-slice_reduce_fusion
  164.5 0.4 copy-done.3
  164.9 0.7 scatter_custom_fusion
  165.7 0.7 gather_fusion
  166.6 0.7 gather_fusion.2
  167.5 85.2 %reduce-scatter.2.cloned.1.call-done = f32[128,2048]{1,0:T(8,128)} async-done(((f32[1024,2048]{1,0:T(8,128)}), f32[128,2048]{1,0:T(8,128)}) %reduce-scatter.2.cloned.1.call-update) | async-done | bytes 1048592 | tf_op jit(solution)/shard_map/reduce_scatter | solution.py:90
  252.8 1.3 copy_bitcast_fusion.1
  254.1 0.7 gather_fusion.1
  254.8 0.3 copy_bitcast_fusion
  255.1 36.0 %all_to_all.5 = f32[16,128,256]{2,1,0:T(8,128)S(1)} all-to-all(f32[16,128,256]{2,1,0:T(8,128)S(1)} %copy_bitcast_fusion), channel_id=1, replica_groups=mesh['grp_0'=2,'grp_1'=4,'blk_0'=2,'blk_1'=4,'blk_2'=2] {'blk_0','blk_1'..., dimensions={0} | all-to-all | bytes 4194304 | tf_op jit(solution)/shard_map/all_to_all | solution.py:109
  291.1 0.3 reduce_sum.18
  291.3 17.6 %all-gather.1 = f32[8,1,256]{2,1,0:T(1,128)S(1)} all-gather(f32[1,1,256]{2,1,0:T(1,128)S(1)} %bitcast.32), channel_id=2, replica_groups=mesh['grp_0'=2,'grp_1'=4,'blk_0'=2,'blk_1'=4,'blk_2'=2] {'grp_0','grp_1'}, dimensions={0}, use_global_device_ids=true | all-gather | bytes 9216 | tf_op jit(solution)/shard_map/all_gather | solution.py:110
  309.0 1.6 divide_bitcast_fusion
  (26 shorter events, 0.8 us)
Async XLA Ops:
  6.5 128.6 %all-gather.4.cloned.1.call-start = ((), (), s32[]{:S(2)}) async-start(), calls=%async_computation.2 | async-start | bytes 17825792 | tf_op jit(solution)/shard_map/all_gather | solution.py:85
  7.9 2.5 copy-start.2
  10.3 242.4 %reduce-scatter.2.cloned.1.call-start = ((), (), s32[]{:S(2)}) async-start(), calls=%async_computation.3 | async-start | bytes 9437184 | tf_op jit(solution)/shard_map/reduce_scatter | solution.py:90
  11.5 2.2 copy-start.1
  135.2 2.2 copy-start
  164.2 0.7 copy-start.3
Sparse Core Ops, SparseCore 0:
  10.5 124.6 all-gather.3
  164.3 88.3 reduce-scatter.1
